TPU v7x, 32 devices: a whole 2x2x4 slice. The times are simulated.
32 devices in a mesh: rep: 2 (over y), fsdp: 16 (over z, x, core).
Axes of the slice: x: 2, y: 2, z: 4, core: 2. Of those that a mesh axis runs over, the one named last changes fastest.
Arguments:
- inputs: bfloat16 [16384, 768], P(('rep', 'fsdp')), may hold values from -6 to 6
- times: float32 [16384], P(('rep', 'fsdp')), may hold values from 0 to 1
- positions: float32 [3, 16384], P(None, ('rep', 'fsdp')), may hold values from -8 to 8
- atom_types: int32 [16384], P(('rep', 'fsdp')), may hold values from 0 to 63
- molecule_ids: int32 [16384], P(('rep', 'fsdp')), may hold values from 0 to 255, never falling along the last dimension, each value on 1 to 128 neighbouring positions
- pad_mask: int32 [16384], P(('rep', 'fsdp')), may hold values 0 or 1
- cotangent: bfloat16 [16384, 768], P(('rep', 'fsdp')), may hold values from -6 to 6
- norm_gains: bfloat16 [2, 768], P(None, 'fsdp'), may hold values from 0.5 to 1.5
- bias_rows: bfloat16 [6, 768], P(None, 'fsdp'), may hold values from -3 to 3
- up_bias: bfloat16 [3072], P('fsdp'), may hold values from -3 to 3
- input_weight: bfloat16 [768, 2304], P(None, 'fsdp'), may hold values from -0.21875 to 0.21875
- output_weight: bfloat16 [768, 768], P(None, 'fsdp'), may hold values from -0.875 to 0.875
- up_weight: bfloat16 [768, 3072], P(None, 'fsdp'), may hold values from -0.21875 to 0.21875
- down_weight: bfloat16 [3072, 768], P(None, 'fsdp'), may hold values from -0.109375 to 0.109375
- kernel_means: bfloat16 [128], P('fsdp'), may hold values from 0 to 6
- kernel_widths: bfloat16 [128], P('fsdp'), may hold values from 0.5 to 3
- pair_scale: bfloat16 [4096], P('fsdp'), may hold values from 0.5 to 1.5
- pair_shift: bfloat16 [4096], P('fsdp'), may hold values from -1 to 1
- kernel_heads: bfloat16 [128, 32], P('fsdp'), may hold values from -3 to 3
Outputs:
- rows: bfloat16 [16384, 768], P(('rep', 'fsdp'))
- inputs_grad: float32 [16384, 768], P(('rep', 'fsdp'))
- norm_gains_grad: float32 [2, 768], P(None, 'fsdp')
- bias_rows_grad: float32 [6, 768], P(None, 'fsdp')
- up_bias_grad: float32 [3072], P('fsdp')
- input_weight_grad: float32 [768, 2304], P(None, 'fsdp')
- output_weight_grad: float32 [768, 768], P(None, 'fsdp')
- up_weight_grad: float32 [768, 3072], P(None, 'fsdp')
- down_weight_grad: float32 [3072, 768], P(None, 'fsdp')
- kernel_means_grad: float32 [128], P('fsdp')
- kernel_widths_grad: float32 [128], P('fsdp')
- pair_scale_grad: float32 [4096], P('fsdp')
- pair_shift_grad: float32 [4096], P('fsdp')
- kernel_heads_grad: float32 [128, 32], P('fsdp')
Inputs may be any that keep to these rules, and one draw needn't show every extreme that they name: `molecule_ids`: molecule ids are non-decreasing along the atoms; a molecule holds 1 to 128 atoms and one holds exactly 128.
All inputs are finite; a program needn't handle non-finite values. No bound on the sum of `pad_mask` on one device may be relied on, other than what follows from the above.
Results may differ from a plain program's by a relative error of at most 0.022.
Values may be sent and summed in bfloat16 or wider, within the bound.
No kernel may reach another device: no remote copies, remote signals or barrier semaphores. Data moves between devices by JAX's collectives and lax.ppermute only.
A program may use at most 128 MiB of HBM per device.

v0:
```python
from functools import partial
import math

import jax
import jax.numpy as jnp
from jax import lax
from jax.sharding import PartitionSpec as P

ATOM_TYPES = 64


epsilon = 1e-05
masked_score = -1000000000.0
time_scale = 1000.0
root_two_pi = math.sqrt(2.0 * math.pi)
highest = lax.Precision.HIGHEST


def time_embedding(times, model_width):
    half_width = model_width // 2
    counter = jnp.arange(half_width, dtype=jnp.float32)
    frequency = jnp.exp(counter * (-math.log(10000.0) / half_width))
    angles = (time_scale * times)[:, None] * frequency[None, :]
    return jnp.concatenate([jnp.sin(angles), jnp.cos(angles)], axis=1)


def layer_norm(values, gain_row, shift_row):
    center = values - jnp.mean(values, axis=1, keepdims=True)
    inv_std = lax.rsqrt(jnp.mean(center * center, axis=1, keepdims=True) + epsilon)
    normed = center * inv_std
    return (normed * gain_row + shift_row, normed, inv_std)


def norm_backward(grad_out, normed, inv_std, gain_row):
    grad_normed = grad_out * gain_row
    first_mean = jnp.mean(grad_normed, axis=1, keepdims=True)
    second_mean = jnp.mean(grad_normed * normed, axis=1, keepdims=True)
    grad_input = inv_std * (grad_normed - first_mean - normed * second_mean)
    return (grad_input, jnp.sum(grad_out * normed, axis=0), jnp.sum(grad_out, axis=0))


def gelu_value(values):
    return values * (0.5 + 0.5 * lax.erf(values * math.sqrt(0.5)))


def gelu_slope(values):
    return (
        0.5
        + 0.5 * lax.erf(values * math.sqrt(0.5))
        + values * jnp.exp(-0.5 * values * values) / root_two_pi
    )


def pair_terms(pos_rows, pos_cols, type_rows, type_cols, tables):
    kernel_means, kernel_widths, scale_table, shift_table = tables
    offsets = pos_rows[:, :, None] - pos_cols[:, None, :]
    distance = jnp.sqrt(jnp.sum(offsets * offsets, axis=0))
    type_range = jnp.arange(ATOM_TYPES, dtype=jnp.int32)
    hot_rows = (type_rows[:, None] == type_range[None, :]).astype(jnp.float32)
    hot_cols = (type_cols[:, None] == type_range[None, :]).astype(jnp.float32)
    scale_pair = jnp.dot(
        jnp.dot(hot_rows, scale_table, precision=highest), hot_cols.T, precision=highest
    )
    shift_pair = jnp.dot(
        jnp.dot(hot_rows, shift_table, precision=highest), hot_cols.T, precision=highest
    )
    stretched = scale_pair * distance + shift_pair
    kernel_gap = (stretched[:, :, None] - kernel_means) / kernel_widths
    kernels = jnp.exp(-0.5 * kernel_gap * kernel_gap) / (root_two_pi * kernel_widths)
    return (distance, hot_rows, hot_cols, kernel_gap, kernels)


def allowed_pairs(row_ids, col_ids, mol_rows, mol_cols, pad_cols):
    same_mol = mol_rows[:, None] == mol_cols[None, :]
    key_live = (pad_cols[None, :] == 1) | (row_ids[:, None] == col_ids[None, :])
    return same_mol & key_live


def tile_scores(q_tile, key_block, kernels_low, kernel_heads, allowed, score_scale):
    pair_bias = jnp.einsum(
        "ijk,kh->hij", kernels_low, kernel_heads, preferred_element_type=jnp.float32
    )
    raw_scores = jnp.einsum("ihd,jhd->hij", q_tile, key_block, preferred_element_type=jnp.float32)
    return jnp.where(allowed[None], raw_scores * score_scale + pair_bias, masked_score)


def block_forward(pieces, tables, kernel_heads, tile_rows):
    queries, key_block, value_block, positions, types, mols, pads = pieces
    block_rows = queries.shape[0]
    score_scale = 1.0 / math.sqrt(queries.shape[2])
    col_ids = jnp.arange(block_rows, dtype=jnp.int32)

    def one_tile(running, tile_index):
        first_row = tile_index * tile_rows
        row_ids = first_row + jnp.arange(tile_rows, dtype=jnp.int32)
        terms = pair_terms(positions, positions, types, types, tables)
        kernels_low = terms[4].astype(jnp.bfloat16)
        allowed = allowed_pairs(row_ids, col_ids, mols, mols, pads)
        scores = tile_scores(queries, key_block, kernels_low, kernel_heads, allowed, score_scale)
        row_max = jnp.max(scores, axis=2, keepdims=True)
        exponent = jnp.exp(scores - row_max)
        row_sum = jnp.sum(exponent, axis=2, keepdims=True)
        probs_low = (exponent / row_sum).astype(jnp.bfloat16)
        attended = jnp.einsum(
            "hij,jhd->ihd", probs_low, value_block, preferred_element_type=jnp.float32
        )
        return (running, (attended, (row_max + jnp.log(row_sum))[:, :, 0]))

    count = block_rows // tile_rows
    _, (attended, log_sums) = lax.scan(one_tile, None, jnp.arange(count, dtype=jnp.int32))
    attended = attended.reshape(block_rows, -1)
    log_sums = jnp.transpose(log_sums, (1, 0, 2)).reshape(log_sums.shape[1], block_rows)
    return (attended, log_sums)


def block_backward(running, pieces, tables, kernel_heads, tile_rows):
    queries, key_block, value_block, grad_attended, log_sums, positions, types, mols, pads = pieces
    kernel_widths = tables[1]
    block_rows = queries.shape[0]
    score_scale = 1.0 / math.sqrt(queries.shape[2])
    col_ids = jnp.arange(block_rows, dtype=jnp.int32)

    def one_tile(partial_sums, tile_index):
        keys_grad, values_grad, heads_grad, means_grad, widths_grad, scale_grad, shift_grad = (
            partial_sums
        )
        first_row = tile_index * tile_rows
        row_ids = first_row + jnp.arange(tile_rows, dtype=jnp.int32)
        distance, hot_rows, hot_cols, kernel_gap, kernels = pair_terms(
            positions, positions, types, types, tables
        )
        kernels_low = kernels.astype(jnp.bfloat16)
        allowed = allowed_pairs(row_ids, col_ids, mols, mols, pads)
        scores = tile_scores(queries, key_block, kernels_low, kernel_heads, allowed, score_scale)
        attn_probs = jnp.exp(scores - log_sums[:, :, None])
        grad_probs = jnp.einsum(
            "ihd,jhd->hij", grad_attended, value_block, preferred_element_type=jnp.float32
        )
        values_grad = values_grad + jnp.einsum(
            "hij,ihd->jhd",
            attn_probs.astype(jnp.bfloat16),
            grad_attended,
            preferred_element_type=jnp.float32,
        )
        probs_dot = jnp.sum(attn_probs * grad_probs, axis=2, keepdims=True)
        grad_scores = (attn_probs * (grad_probs - probs_dot)).astype(jnp.bfloat16)
        query_grad = (
            jnp.einsum("hij,jhd->ihd", grad_scores, key_block, preferred_element_type=jnp.float32)
            * score_scale
        )
        keys_grad = (
            keys_grad
            + jnp.einsum("hij,ihd->jhd", grad_scores, queries, preferred_element_type=jnp.float32)
            * score_scale
        )
        heads_grad = heads_grad + jnp.einsum(
            "ijk,hij->kh", kernels_low, grad_scores, preferred_element_type=jnp.float32
        )
        grad_kernels = jnp.einsum(
            "hij,kh->ijk", grad_scores, kernel_heads, preferred_element_type=jnp.float32
        )
        spread = grad_kernels * kernels
        mean_part = spread * kernel_gap / kernel_widths
        means_grad = means_grad + jnp.sum(mean_part, axis=(0, 1))
        widths_grad = widths_grad + jnp.sum(
            spread * (kernel_gap * kernel_gap - 1.0) / kernel_widths, axis=(0, 1)
        )
        grad_stretched = -jnp.sum(mean_part, axis=2)
        scale_grad = scale_grad + jnp.dot(
            jnp.dot(hot_rows.T, grad_stretched * distance, precision=highest),
            hot_cols,
            precision=highest,
        )
        shift_grad = shift_grad + jnp.dot(
            jnp.dot(hot_rows.T, grad_stretched, precision=highest), hot_cols, precision=highest
        )
        return (
            (keys_grad, values_grad, heads_grad, means_grad, widths_grad, scale_grad, shift_grad),
            query_grad,
        )

    zero_block = jnp.zeros(key_block.shape, jnp.float32)
    count = block_rows // tile_rows
    sums_out, query_grads = lax.scan(
        one_tile, (zero_block, zero_block) + tuple(running), jnp.arange(count, dtype=jnp.int32)
    )
    query_grads = query_grads.reshape(key_block.shape)
    return (sums_out[2:], (query_grads, sums_out[0], sums_out[1]))


def unpack(weights):
    gains_now = weights[0].astype(jnp.float32)
    biases_now = weights[1].astype(jnp.float32)
    up_shift = weights[2].astype(jnp.float32)
    tables = (
        weights[7].astype(jnp.float32),
        weights[8].astype(jnp.float32),
        weights[9].astype(jnp.float32).reshape(ATOM_TYPES, ATOM_TYPES),
        weights[10].astype(jnp.float32).reshape(ATOM_TYPES, ATOM_TYPES),
    )
    return (
        gains_now,
        biases_now,
        up_shift,
        weights[3],
        weights[4],
        weights[5],
        weights[6],
        tables,
        weights[11],
    )


def body(
    inputs,
    times,
    positions,
    atom_types,
    molecule_ids,
    pad_mask,
    cotangent,
    norm_gains,
    bias_rows,
    up_bias,
    input_weight,
    output_weight,
    up_weight,
    down_weight,
    kernel_means,
    kernel_widths,
    pair_scale,
    pair_shift,
    kernel_heads,
):
    gathered = (
        lax.all_gather(norm_gains, "fsdp", axis=1, tiled=True),
        lax.all_gather(bias_rows, "fsdp", axis=1, tiled=True),
        lax.all_gather(up_bias, "fsdp", axis=0, tiled=True),
        lax.all_gather(input_weight, "fsdp", axis=1, tiled=True),
        lax.all_gather(output_weight, "fsdp", axis=1, tiled=True),
        lax.all_gather(up_weight, "fsdp", axis=1, tiled=True),
        lax.all_gather(down_weight, "fsdp", axis=1, tiled=True),
        lax.all_gather(kernel_means, "fsdp", axis=0, tiled=True),
        lax.all_gather(kernel_widths, "fsdp", axis=0, tiled=True),
        lax.all_gather(pair_scale, "fsdp", axis=0, tiled=True),
        lax.all_gather(pair_shift, "fsdp", axis=0, tiled=True),
        lax.all_gather(kernel_heads, "fsdp", axis=0, tiled=True),
    )
    row_count = inputs.shape[0]
    model_width = inputs.shape[1]
    head_count = kernel_heads.shape[1]
    head_size = model_width // head_count
    block_rows = min(128, row_count)
    blocks = row_count // block_rows
    tile_rows = min(128, block_rows)
    gains_now, biases_now, up_shift, in_full, out_full, up_full, down_full, tables, heads_full = (
        unpack(gathered)
    )
    stream = inputs.astype(jnp.float32) + time_embedding(times, model_width)
    normed_out, normed_one, inv_one = layer_norm(stream, gains_now[0], biases_now[0])
    act_one = normed_out.astype(jnp.bfloat16)
    qkv_shift = jnp.concatenate([biases_now[2], jnp.zeros_like(biases_now[2]), biases_now[3]])
    projected = (jnp.dot(act_one, in_full, preferred_element_type=jnp.float32) + qkv_shift).astype(
        jnp.bfloat16
    )
    split_shape = (blocks, block_rows, head_count, head_size)
    queries = projected[:, :model_width].reshape(split_shape)
    key_rows = projected[:, model_width : 2 * model_width].reshape(split_shape)
    value_rows = projected[:, 2 * model_width :].reshape(split_shape)
    pos_blocks = jnp.transpose(positions.reshape(3, blocks, block_rows), (1, 0, 2))
    type_blocks = atom_types.reshape(blocks, block_rows)
    mol_blocks = molecule_ids.reshape(blocks, block_rows)
    pad_blocks = pad_mask.reshape(blocks, block_rows)
    attended, log_sums = lax.map(
        partial(block_forward, tables=tables, kernel_heads=heads_full, tile_rows=tile_rows),
        (queries, key_rows, value_rows, pos_blocks, type_blocks, mol_blocks, pad_blocks),
    )
    attended_low = attended.reshape(row_count, model_width).astype(jnp.bfloat16)
    mid = stream + (
        jnp.dot(attended_low, out_full, preferred_element_type=jnp.float32) + biases_now[4]
    )
    normed_out_two, normed_two, inv_two = layer_norm(mid, gains_now[1], biases_now[1])
    act_two = normed_out_two.astype(jnp.bfloat16)
    hidden_pre = jnp.dot(act_two, up_full, preferred_element_type=jnp.float32) + up_shift
    hidden_low = gelu_value(hidden_pre).astype(jnp.bfloat16)
    final = mid + (
        jnp.dot(hidden_low, down_full, preferred_element_type=jnp.float32) + biases_now[5]
    )
    rows_out = final.astype(jnp.bfloat16)
    weights_back = (
        lax.all_gather(norm_gains, "fsdp", axis=1, tiled=True),
        lax.all_gather(bias_rows, "fsdp", axis=1, tiled=True),
        lax.all_gather(up_bias, "fsdp", axis=0, tiled=True),
        lax.all_gather(input_weight, "fsdp", axis=1, tiled=True),
        lax.all_gather(output_weight, "fsdp", axis=1, tiled=True),
        lax.all_gather(up_weight, "fsdp", axis=1, tiled=True),
        lax.all_gather(down_weight, "fsdp", axis=1, tiled=True),
        lax.all_gather(kernel_means, "fsdp", axis=0, tiled=True),
        lax.all_gather(kernel_widths, "fsdp", axis=0, tiled=True),
        lax.all_gather(pair_scale, "fsdp", axis=0, tiled=True),
        lax.all_gather(pair_shift, "fsdp", axis=0, tiled=True),
        lax.all_gather(kernel_heads, "fsdp", axis=0, tiled=True),
    )
    (
        gains_back,
        biases_back,
        up_unused,
        in_back,
        out_back,
        up_back,
        down_back,
        tables_back,
        heads_back,
    ) = unpack(weights_back)
    grad_final = cotangent.astype(jnp.float32)
    down_grad = jnp.einsum("nf,nd->fd", hidden_low, cotangent, preferred_element_type=jnp.float32)
    grad_hidden = jnp.einsum(
        "nd,fd->nf", cotangent, down_back, preferred_element_type=jnp.float32
    ) * gelu_slope(hidden_pre)
    grad_hidden_low = grad_hidden.astype(jnp.bfloat16)
    up_grad = jnp.einsum("nd,nf->df", act_two, grad_hidden_low, preferred_element_type=jnp.float32)
    up_bias_grad = jnp.sum(grad_hidden_low.astype(jnp.float32), axis=0)
    grad_act_two = jnp.einsum(
        "nf,df->nd", grad_hidden_low, up_back, preferred_element_type=jnp.float32
    )
    grad_norm_two, gain_two_grad, shift_two_grad = norm_backward(
        grad_act_two, normed_two, inv_two, gains_back[1]
    )
    grad_mid = grad_final + grad_norm_two
    grad_branch_low = grad_mid.astype(jnp.bfloat16)
    out_grad = jnp.einsum(
        "nd,ne->de", attended_low, grad_branch_low, preferred_element_type=jnp.float32
    )
    grad_attended = jnp.einsum(
        "ne,de->nd", grad_branch_low, out_back, preferred_element_type=jnp.float32
    ).astype(jnp.bfloat16)
    kernel_count = tables_back[0].shape[0]
    start_sums = (
        jnp.zeros((kernel_count, head_count), jnp.float32),
        jnp.zeros((kernel_count,), jnp.float32),
        jnp.zeros((kernel_count,), jnp.float32),
        jnp.zeros((ATOM_TYPES, ATOM_TYPES), jnp.float32),
        jnp.zeros((ATOM_TYPES, ATOM_TYPES), jnp.float32),
    )
    kernel_sums, (queries_grad, keys_grad, values_grad) = lax.scan(
        partial(block_backward, tables=tables_back, kernel_heads=heads_back, tile_rows=tile_rows),
        start_sums,
        (
            queries,
            key_rows,
            value_rows,
            grad_attended.reshape(split_shape),
            log_sums,
            pos_blocks,
            type_blocks,
            mol_blocks,
            pad_blocks,
        ),
    )
    grad_projected = jnp.concatenate(
        [
            queries_grad.reshape(row_count, model_width),
            keys_grad.reshape(row_count, model_width),
            values_grad.reshape(row_count, model_width),
        ],
        axis=1,
    ).astype(jnp.bfloat16)
    input_weight_grad = jnp.einsum(
        "nd,ne->de", act_one, grad_projected, preferred_element_type=jnp.float32
    )
    grad_act_one = jnp.einsum(
        "ne,de->nd", grad_projected, in_back, preferred_element_type=jnp.float32
    )
    grad_norm_one, gain_one_grad, shift_one_grad = norm_backward(
        grad_act_one, normed_one, inv_one, gains_back[0]
    )
    inputs_grad = grad_mid + grad_norm_one
    projected_sums = jnp.sum(grad_projected.astype(jnp.float32), axis=0)
    gains_grad = jnp.stack([gain_one_grad, gain_two_grad])
    biases_grad = jnp.stack(
        [
            shift_one_grad,
            shift_two_grad,
            projected_sums[:model_width],
            projected_sums[2 * model_width :],
            jnp.sum(grad_branch_low.astype(jnp.float32), axis=0),
            jnp.sum(grad_final, axis=0),
        ]
    )
    heads_grad, means_grad, widths_grad, scale_grad, shift_grad = kernel_sums
    owned = (
        lax.psum_scatter(gains_grad, "fsdp", scatter_dimension=1, tiled=True),
        lax.psum_scatter(biases_grad, "fsdp", scatter_dimension=1, tiled=True),
        lax.psum_scatter(up_bias_grad, "fsdp", scatter_dimension=0, tiled=True),
        lax.psum_scatter(input_weight_grad, "fsdp", scatter_dimension=1, tiled=True),
        lax.psum_scatter(out_grad, "fsdp", scatter_dimension=1, tiled=True),
        lax.psum_scatter(up_grad, "fsdp", scatter_dimension=1, tiled=True),
        lax.psum_scatter(down_grad, "fsdp", scatter_dimension=1, tiled=True),
        lax.psum_scatter(means_grad, "fsdp", scatter_dimension=0, tiled=True),
        lax.psum_scatter(widths_grad, "fsdp", scatter_dimension=0, tiled=True),
        lax.psum_scatter(scale_grad.reshape(-1), "fsdp", scatter_dimension=0, tiled=True),
        lax.psum_scatter(shift_grad.reshape(-1), "fsdp", scatter_dimension=0, tiled=True),
        lax.psum_scatter(heads_grad, "fsdp", scatter_dimension=0, tiled=True),
    )
    totals = (
        lax.psum(owned[0].astype(jnp.bfloat16), "rep").astype(jnp.float32),
        lax.psum(owned[1].astype(jnp.bfloat16), "rep").astype(jnp.float32),
        lax.psum(owned[2].astype(jnp.bfloat16), "rep").astype(jnp.float32),
        lax.psum(owned[3].astype(jnp.bfloat16), "rep").astype(jnp.float32),
        lax.psum(owned[4].astype(jnp.bfloat16), "rep").astype(jnp.float32),
        lax.psum(owned[5].astype(jnp.bfloat16), "rep").astype(jnp.float32),
        lax.psum(owned[6].astype(jnp.bfloat16), "rep").astype(jnp.float32),
        lax.psum(owned[7].astype(jnp.bfloat16), "rep").astype(jnp.float32),
        lax.psum(owned[8].astype(jnp.bfloat16), "rep").astype(jnp.float32),
        lax.psum(owned[9].astype(jnp.bfloat16), "rep").astype(jnp.float32),
        lax.psum(owned[10].astype(jnp.bfloat16), "rep").astype(jnp.float32),
        lax.psum(owned[11].astype(jnp.bfloat16), "rep").astype(jnp.float32),
    )
    return (
        rows_out,
        inputs_grad,
        totals[0],
        totals[1],
        totals[2],
        totals[3],
        totals[4],
        totals[5],
        totals[6],
        totals[7],
        totals[8],
        totals[9],
        totals[10],
        totals[11],
    )


def solution(mesh):
    placed = (
        P(("rep", "fsdp"), None),
        P(("rep", "fsdp")),
        P(None, ("rep", "fsdp")),
        P(("rep", "fsdp")),
        P(("rep", "fsdp")),
        P(("rep", "fsdp")),
        P(("rep", "fsdp"), None),
        P(None, "fsdp"),
        P(None, "fsdp"),
        P("fsdp"),
        P(None, "fsdp"),
        P(None, "fsdp"),
        P(None, "fsdp"),
        P(None, "fsdp"),
        P("fsdp"),
        P("fsdp"),
        P("fsdp"),
        P("fsdp"),
        P("fsdp", None),
    )
    return jax.shard_map(
        body,
        mesh=mesh,
        in_specs=placed,
        out_specs=(
            P(("rep", "fsdp"), None),
            P(("rep", "fsdp"), None),
            P(None, "fsdp"),
            P(None, "fsdp"),
            P("fsdp"),
            P(None, "fsdp"),
            P(None, "fsdp"),
            P(None, "fsdp"),
            P(None, "fsdp"),
            P("fsdp"),
            P("fsdp"),
            P("fsdp"),
            P("fsdp"),
            P("fsdp", None),
        ),
        check_vma=False,
    )
```

profile of v0, /device:TPU:0, one launch (start us, length us, event | category | flops | bytes accessed | tf_op | source)
XLA Modules:
  0.0 911.3 jit_solution(4812021375937304836)
XLA Ops:
  10.8 23.5 %all-gather.1 = bf16[16,48,6]{1,2,0:T(8,128)(2,1)S(1)} all-gather(bf16[1,48,6]{1,2,0:T(8,128)(2,1)} %bitcast.283), channel_id=1, replica_groups=mesh['rep'=2,'fsdp'=16] {'fsdp'}, dimensions={0}, use_global_device_ids=true | all-gather | bytes 9792 | tf_op jit(solution)/shard_map/all_gather | solution.py:237
  35.1 17.8 %all-gather = bf16[16,48,2]{1,2,0:T(2,128)(2,1)S(1)} all-gather(bf16[1,48,2]{1,2,0:T(2,128)(2,1)} %bitcast.284), channel_id=1, replica_groups=mesh['rep'=2,'fsdp'=16] {'fsdp'}, dimensions={0}, use_global_device_ids=true | all-gather | bytes 3264 | tf_op jit(solution)/shard_map/all_gather | solution.py:236
  53.6 2.8 multiply_sine_fusion
  57.1 19.0 %all-gather.2 = bf16[16,1,256]{2,1,0:T(2,128)(2,1)S(1)} all-gather(bf16[1,1,256]{2,1,0:T(2,128)(2,1)S(1)} %reshape.402), channel_id=1, replica_groups=mesh['rep'=2,'fsdp'=16] {'fsdp'}, dimensions={0}, use_global_device_ids=true | all-gather | bytes 8704 | tf_op jit(solution)/shard_map/all_gather | solution.py:245
  76.2 17.5 %all-gather.3 = bf16[16,1,256]{2,1,0:T(2,128)(2,1)S(1)} all-gather(bf16[1,1,256]{2,1,0:T(2,128)(2,1)S(1)} %reshape.404), channel_id=1, replica_groups=mesh['rep'=2,'fsdp'=16] {'fsdp'}, dimensions={0}, use_global_device_ids=true | all-gather | bytes 8704 | tf_op jit(solution)/shard_map/all_gather | solution.py:246
  96.4 32.1 %all-reduce.10 = (bf16[128]{0:T(256)(128)(2,1)S(1)}, bf16[128]{0:T(256)(128)(2,1)S(1)}, bf16[3072]{0:T(1024)(128)(2,1)S(1)}) all-reduce(bf16[128]{0:T(256)(128)(2,1)S(1)} %dynamic-update-slice, bf16[128]{0:T(256)(128)(2,1)S(1)} %dynamic-update-slice.1, bf16[3072]{0:T(1024)(128)(2,1)S(1)} %dynamic-update-slice.2), channel_id=1, replica_groups=mesh['rep'=2,'fsdp'=16] {'fsdp'}, use_global_device_ids=true, to_apply=%add | all-reduce | flops 3328 | bytes 13312
  128.6 18.2 %all_gather.53 = bf16[128,32]{1,0:T(8,128)(2,1)S(1)} all-gather(bf16[8,32]{1,0:T(8,128)(2,1)S(1)} %copy-done.56), channel_id=1, replica_groups=mesh['rep'=2,'fsdp'=16] {'fsdp'}, dimensions={0}, use_global_device_ids=true | all-gather | bytes 8704 | tf_op jit(solution)/shard_map/all_gather | solution.py:247
  147.6 4.1 fusion.107
  158.3 57.5 %while.41 = (s32[]{:T(128)}, bf16[4,128,768]{2,1,0:T(8,128)(2,1)}, f32[4,32,128]{2,1,0:T(8,128)S(1)}, bf16[4,128,32,24]{1,3,2,0:T(8,128)(2,1)}, s32[4,128]{1,0:T...) while((s32[]{:T(128)}, bf16[4,128,768]{2,1,0:T(8,128)(2,1)}, ...), condition=%wide.region_6.7_spmd, body=%wide.region_2.6_spmd.sunk | while | flops 239857920 | bytes 16995764 | solution.py:274
  160.3 5.4 fusion.219
  165.7 2.0 copy.199
  174.7 5.4 fusion.219
  180.0 2.0 copy.199
  189.0 5.4 fusion.219
  194.4 2.0 copy.199
  203.5 5.4 fusion.219
  208.8 2.0 copy.199
  215.9 2.9 fusion.120
  219.2 7.3 multiply_convert_fusion.1
  226.6 22.2 %convert_reduce_fusion = (f32[3072]{0:T(1024)}, bf16[512,3072]{1,0:T(8,128)(2,1)S(1)}) fusion(f32[512,3072]{1,0:T(8,128)} %get-tuple-element.1023, f32[3072]{0:T(1024)S(1)} %copy-done.42, bf16[512,768]{1,0:T(8,128)(2,1)} %param.29, bf16[3072,768]{0,1:T(8,128)(2,1)} %all-gather.15.cloned.1.call-done), kind=kOutput, calls=%fused_computation.144 | convolution fusion | flops 2436363264 | bytes 14966784 | tf_op jit(solution)/shard_map/nd,fd->nf/dot_general | solution.py:317
  248.7 3.4 multiply_reduce_fusion.3
  252.2 2.8 convert_reduce_fusion.3
  255.0 2.2 fusion.108
  257.2 2.9 convolution_convert_fusion
  262.9 147.5 %while.42 = (s32[]{:T(128)}, f32[128,32]{0,1:T(8,128)S(1)}, f32[128]{0:T(128)S(1)}, f32[128]{0:T(128)S(1)}, f32[64,64]{1,0:T(8,128)S(1)}, /*index=5*/f32[64,64]{...) while((s32[]{:T(128)}, f32[128,32]{0,1:T(8,128)S(1)}, ...), condition=%wide.region_17.18_spmd.clone, body=%wide.region_11.17_spmd.clone.sunk | while | flops 666391040 | bytes 86731560 | solution.py:345
  263.0 3.1 fusion.245
  267.4 2.4 fusion.250
  273.2 3.4 multiply_reduce_fusion.16
  278.8 6.2 fusion.253
  285.0 5.3 fusion.254
  290.3 2.3 fusion.255
  297.0 1.9 fusion.261
  299.8 3.1 fusion.245
  304.2 2.4 fusion.250
  310.0 3.4 multiply_reduce_fusion.16
  315.6 6.2 fusion.253
  321.8 5.3 fusion.254
  327.1 2.3 fusion.255
  336.6 3.1 fusion.245
  341.0 2.4 fusion.250
  346.8 3.3 multiply_reduce_fusion.16
  352.3 6.2 fusion.253
  358.5 5.3 fusion.254
  363.8 2.3 fusion.255
  373.3 3.1 fusion.245
  377.7 2.4 fusion.250
  383.5 3.3 multiply_reduce_fusion.16
  389.0 6.2 fusion.253
  395.2 5.3 fusion.254
  400.5 2.3 fusion.255
  415.4 5.1 fusion.111
  421.9 8.7 fusion.112
  431.8 7.5 fusion.121
  441.4 6.2 multiply_reduce_fusion.4
  448.6 2.4 convert_reduce_fusion.1
  452.5 3.1 multiply_add_fusion.1
  455.8 63.0 %all-reduce.9 = (bf16[3072]{0:T(1024)(128)(2,1)S(1)}, bf16[128]{0:T(256)(128)(2,1)S(1)}, bf16[128]{0:T(256)(128)(2,1)S(1)}, bf16[4096]{0:T(1024)(128)(2,1)S(1)},...) all-reduce(f32[3072]{0:T(1024)S(1)} %copy-done.41, ...), channel_id=4, replica_groups=mesh['rep'=2,'fsdp'=16] {'fsdp'}, use_global_device_ids=true, to_apply=%region_32.33.clone | all-reduce | flops 15616 | bytes 93696
  522.5 102.8 %reduce-scatter.15.cloned.1.call-done = f32[768,192]{0,1:T(8,128)} async-done(((f32[768,3072]{0,1:T(8,128)}), f32[768,192]{0,1:T(8,128)}) %reduce-scatter.15.cloned.1.call-update) | async-done | bytes 589840 | tf_op jit(solution)/shard_map/reduce_scatter | solution.py:397
  627.1 113.2 %reduce-scatter.17.cloned.1.call-done = f32[3072,48]{0,1:T(8,128)} async-done(((f32[3072,768]{0,1:T(8,128)}), f32[3072,48]{0,1:T(8,128)}) %reduce-scatter.17.cloned.1.call-update) | async-done | bytes 589840 | tf_op jit(solution)/shard_map/reduce_scatter | solution.py:398
  742.2 6.8 add_convert_fusion
  749.0 51.0 %reduce-scatter.19.cloned.1.call-done = f32[48,2]{1,0:T(8,128)} async-done(((f32[768,2]{1,0:T(8,128)}), f32[48,2]{1,0:T(8,128)}) %reduce-scatter.19.cloned.1.call-update) | async-done | bytes 400
  800.8 58.2 %reduce-scatter.21.cloned.1.call-done = f32[48,6]{1,0:T(8,128)} async-done(((f32[768,6]{1,0:T(8,128)}), f32[48,6]{1,0:T(8,128)}) %reduce-scatter.21.cloned.1.call-update) | async-done | bytes 1168
  859.8 5.0 all-reduce.11
  869.3 28.5 %all-reduce.15.cloned.1.call-done = (bf16[768,144]{0,1:T(8,128)(2,1)}, bf16[768,48]{0,1:T(8,128)(2,1)}, bf16[768,192]{0,1:T(8,128)(2,1)}, bf16[3072,48]{0,1:T(8,128)(2,1)}) async-done(((bf16[768,144]{0,1:T(8,128)(2,1)}, bf16[768,48]{0,1:T(8,128)(2,1)}, bf16[768,192]{0,1:T(8,128)(2,1)}, bf16[3072,48]{0,1:T(8,128)(2,1)}), (bf16[768,144]{0,1:T(8,128)(2,1)}, bf16[768,48]{0,1:T(8,128)(2,1)}, ...) | async-done | bytes 884752 | tf_op jit(solution)/shard_map/psum | solution.py:409
  (479 shorter events, 129.1 us)
Async XLA Ops:
  7.2 49.2 %copy-start.15 = (bf16[512,768]{1,0:T(8,128)(2,1)S(1)}, bf16[512,768]{1,0:T(8,128)(2,1)}, u32[]{:S(2)}) copy-start(bf16[512,768]{1,0:T(8,128)(2,1)} %param.23) | copy-start | bytes 2359300
  7.2 140.4 %all-gather.9.cloned.1.call-start = ((), (), s32[]{:S(2)}) async-start(), calls=%async_computation.6 | async-start | bytes 3760128 | tf_op jit(solution)/shard_map/all_gather | solution.py:239
  7.9 208.0 %all-gather.11.cloned.1.call-start = ((), (), s32[]{:S(2)}) async-start(), calls=%async_computation.7 | async-start | bytes 1253376 | tf_op jit(solution)/shard_map/all_gather | solution.py:240
  8.7 210.5 %all-gather.13.cloned.1.call-start = ((), (), s32[]{:S(2)}) async-start(), calls=%async_computation.8 | async-start | bytes 5013504 | tf_op jit(solution)/shard_map/all_gather | solution.py:241
  9.4 217.2 %all-gather.15.cloned.1.call-start = ((), (), s32[]{:S(2)}) async-start(), calls=%async_computation.9 | async-start | bytes 5013504 | tf_op jit(solution)/shard_map/all_gather | solution.py:242
  10.0 509.2 %reduce-scatter.13.cloned.1.call-start = ((), (), s32[]{:S(2)}) async-start(), calls=%async_computation.11 | async-start | bytes 2506752 | tf_op jit(solution)/shard_map/reduce_scatter | solution.py:396
  35.1 112.5 %copy-start.52 = (f32[768]{0:T(1024)}, f32[768]{0:T(1024)S(1)}, u32[]{:S(2)}) copy-start(f32[768]{0:T(1024)S(1)} %get-tuple-element.896) | copy-start | bytes 9220
  53.6 94.0 %copy-start.39 = (f32[768]{0:T(1024)}, f32[768]{0:T(1024)S(1)}, u32[]{:S(2)}) copy-start(f32[768]{0:T(1024)S(1)} %get-tuple-element.898) | copy-start | bytes 9220
  56.4 19.8 %copy-start.60 = (bf16[256]{0:T(256)(128)(2,1)S(1)}, bf16[256]{0:T(256)(128)(2,1)}, u32[]{:S(2)}) copy-start(bf16[256]{0:T(256)(128)(2,1)} %param.40) | copy-start | bytes 1540
  56.4 37.3 %copy-start.57 = (u32[32]{0:T(128)S(1)}, u32[32]{0:T(128)}, u32[]{:S(2)}) copy-start(u32[32]{0:T(128)} %constant.211) | copy-start | bytes 388
  56.4 39.2 %copy-start.61 = (bf16[8]{0:T(256)(128)(2,1)S(1)}, bf16[8]{0:T(256)(128)(2,1)}, u32[]{:S(2)}) copy-start(bf16[8]{0:T(256)(128)(2,1)} %param.37) | copy-start | bytes 52
  56.4 39.5 %copy-start.62 = (bf16[8]{0:T(256)(128)(2,1)S(1)}, bf16[8]{0:T(256)(128)(2,1)}, u32[]{:S(2)}) copy-start(bf16[8]{0:T(256)(128)(2,1)} %param.38) | copy-start | bytes 52
  56.4 39.7 %copy-start.63 = (bf16[192]{0:T(256)(128)(2,1)S(1)}, bf16[192]{0:T(256)(128)(2,1)}, u32[]{:S(2)}) copy-start(bf16[192]{0:T(256)(128)(2,1)} %param.32) | copy-start | bytes 1156
  56.5 72.1 %copy-start.56 = (bf16[8,32]{1,0:T(8,128)(2,1)S(1)}, bf16[8,32]{1,0:T(8,128)(2,1)}, u32[]{:S(2)}) copy-start(bf16[8,32]{1,0:T(8,128)(2,1)} %param.41) | copy-start | bytes 1540
  56.7 95.0 %copy-start.4 = (f32[512,768]{1,0:T(8,128)}, f32[512,768]{1,0:T(8,128)S(1)}, u32[]{:S(2)}) copy-start(f32[512,768]{1,0:T(8,128)S(1)} %get-tuple-element.999) | copy-start | bytes 4718596
  56.7 95.0 %copy-start.28 = (f32[512]{0:T(512)}, f32[512]{0:T(512)S(1)}, u32[]{:S(2)}) copy-start(f32[512]{0:T(512)S(1)} %broadcast_multiply_fusion.7) | copy-start | bytes 6148
  57.1 94.7 %copy-start.43 = (f32[512]{0:T(512)}, f32[512]{0:T(512)S(1)}, u32[]{:S(2)}) copy-start(f32[512]{0:T(512)S(1)} %add_rsqrt_fusion.1) | copy-start | bytes 6148
  158.3 57.6 %copy-start.54 = (f32[768]{0:T(1024)S(1)}, f32[768]{0:T(1024)}, u32[]{:S(2)}) copy-start(f32[768]{0:T(1024)} %get-tuple-element.893) | copy-start | bytes 9220
  215.9 3.3 copy-start.34
  215.9 3.3 copy-start.42
  215.9 3.3 copy-start.50
  218.8 29.9 %copy-start.8 = (f32[512,768]{1,0:T(8,128)}, f32[512,768]{1,0:T(8,128)S(1)}, u32[]{:S(2)}) copy-start(f32[512,768]{1,0:T(8,128)S(1)} %get-tuple-element.1021) | copy-start | bytes 4718596
  218.9 33.3 %copy-start.30 = (f32[512]{0:T(512)}, f32[512]{0:T(512)S(1)}, u32[]{:S(2)}) copy-start(f32[512]{0:T(512)S(1)} %broadcast_multiply_fusion.6) | copy-start | bytes 6148
  219.2 33.0 %copy-start.45 = (f32[512]{0:T(512)}, f32[512]{0:T(512)S(1)}, u32[]{:S(2)}) copy-start(f32[512]{0:T(512)S(1)} %add_rsqrt_fusion) | copy-start | bytes 6148
  226.6 22.2 %copy-start.58 = (bf16[768,3072]{0,1:T(8,128)(2,1)S(1)}, bf16[768,3072]{0,1:T(8,128)(2,1)}, u32[]{:S(2)}) copy-start(bf16[768,3072]{0,1:T(8,128)(2,1)} %all-gather.13.cloned.1.call-done) | copy-start | bytes 14155780
  248.7 3.4 copy-start.64
  248.7 3.5 copy-start.16
  262.8 257.9 %reduce-scatter.11.cloned.1.call-start = ((), (), s32[]{:S(2)}) async-start(), calls=%async_computation.10 | async-start | bytes 7520256 | tf_op jit(solution)/shard_map/reduce_scatter | solution.py:395
  262.9 10.2 %copy-start.2 = (bf16[4,128,32,24]{1,3,2,0:T(8,128)(2,1)}, bf16[4,128,32,24]{1,3,2,0:T(8,128)(2,1)S(1)}, u32[]{:S(2)}) copy-start(bf16[4,128,32,24]{1,3,2,0:T(8,128)(2,1)S(1)} %get-tuple-element.1399) | copy-start | bytes 2359300 | tf_op jit(solution)/shard_map/while
  273.1 3.5 copy-start
  278.8 6.2 copy-start.1
  290.3 3.4 copy-start.19
  292.6 4.4 copy-start.24
  295.0 3.8 copy-start.20
  299.8 10.2 %copy-start.2 = (bf16[4,128,32,24]{1,3,2,0:T(8,128)(2,1)}, bf16[4,128,32,24]{1,3,2,0:T(8,128)(2,1)S(1)}, u32[]{:S(2)}) copy-start(bf16[4,128,32,24]{1,3,2,0:T(8,128)(2,1)S(1)} %get-tuple-element.1399) | copy-start | bytes 2359300 | tf_op jit(solution)/shard_map/while
  310.0 3.4 copy-start
  315.6 6.2 copy-start.1
  327.1 3.4 copy-start.19
  329.4 4.4 copy-start.24
  331.9 3.8 copy-start.20
  336.6 10.2 %copy-start.2 = (bf16[4,128,32,24]{1,3,2,0:T(8,128)(2,1)}, bf16[4,128,32,24]{1,3,2,0:T(8,128)(2,1)S(1)}, u32[]{:S(2)}) copy-start(bf16[4,128,32,24]{1,3,2,0:T(8,128)(2,1)S(1)} %get-tuple-element.1399) | copy-start | bytes 2359300 | tf_op jit(solution)/shard_map/while
  346.8 3.3 copy-start
  352.3 6.2 copy-start.1
  363.8 3.4 copy-start.19
  366.1 4.4 copy-start.24
  368.6 3.8 copy-start.20
  373.3 10.2 %copy-start.2 = (bf16[4,128,32,24]{1,3,2,0:T(8,128)(2,1)}, bf16[4,128,32,24]{1,3,2,0:T(8,128)(2,1)S(1)}, u32[]{:S(2)}) copy-start(bf16[4,128,32,24]{1,3,2,0:T(8,128)(2,1)S(1)} %get-tuple-element.1399) | copy-start | bytes 2359300 | tf_op jit(solution)/shard_map/while
  383.5 3.3 copy-start
  389.0 6.2 copy-start.1
  400.5 3.4 copy-start.19
  402.8 4.4 copy-start.24
  405.3 3.8 copy-start.20
  420.6 204.7 %reduce-scatter.15.cloned.1.call-start = ((), (), s32[]{:S(2)}) async-start(), calls=%async_computation.12 | async-start | bytes 10027008 | tf_op jit(solution)/shard_map/reduce_scatter | solution.py:397
  430.7 309.6 %reduce-scatter.17.cloned.1.call-start = ((), (), s32[]{:S(2)}) async-start(), calls=%async_computation.13 | async-start | bytes 10027008 | tf_op jit(solution)/shard_map/reduce_scatter | solution.py:398
  439.4 360.7 %reduce-scatter.19.cloned.1.call-start = ((), (), s32[]{:S(2)}) async-start(), calls=%async_computation.14 | async-start | bytes 417792
  447.6 3.5 copy-start.47
  447.6 3.6 copy-start.37
  447.6 3.6 copy-start.36
  447.6 4.8 copy-start.7
  451.1 407.9 %reduce-scatter.21.cloned.1.call-start = ((), (), s32[]{:S(2)}) async-start(), calls=%async_computation.15 | async-start | bytes 417792
  452.2 445.5 %all-reduce.15.cloned.1.call-start = ((), (), s32[]{:S(2)}) async-start(), calls=%async_computation.16 | async-start | bytes 1769472 | tf_op jit(solution)/shard_map/psum | solution.py:409
  452.5 3.3 copy-start.41
  455.5 286.6 %copy-start.10 = (f32[512,768]{1,0:T(8,128)S(1)}, f32[512,768]{1,0:T(8,128)}, u32[]{:S(2)}) copy-start(f32[512,768]{1,0:T(8,128)} %copy-done.8) | copy-start | bytes 4718596
  455.5 286.6 %copy-start.49 = (f32[768]{0:T(1024)S(1)}, f32[768]{0:T(1024)}, u32[]{:S(2)}) copy-start(f32[768]{0:T(1024)} %get-tuple-element.891) | copy-start | bytes 9220
  (42 other events, 75.0 us)
Sparse Core Ops, SparseCore 0:
  10.3 49.8 all-gather.8
  62.4 36.9 all-gather.10
  101.7 52.2 all-gather.12
  156.2 51.7 all-gather.14
  263.0 62.0 reduce-scatter.12
  420.7 90.0 reduce-scatter.10
  514.9 110.3 reduce-scatter.14
  629.4 110.8 reduce-scatter.16
  744.4 55.6 reduce-scatter.18
  803.9 55.0 reduce-scatter.20
  862.1 35.5 all-reduce.14
where the time goes:
time: 919 us; the launch traced here: 911 us
  waiting for transfers between devices  356 us (39%)
  matrix products  228 us (25%)
  blocking collectives  196 us (21%)
  local copies, waits for them, and re-layouts  58.9 us (6%)
  other arithmetic  51.6 us (6%)
  between operations  18.3 us (2%)
    reduce_scatter x1, waiting for transfers between devices, body(): lax.psum_scatter(down_grad, 'fsdp', scatter_dimension=1, tiled=True)  113 us
    unnamed x13, waiting for transfers between devices  112 us
    reduce_scatter x1, waiting for transfers between devices, body(): lax.psum_scatter(up_grad, 'fsdp', scatter_dimension=1, tiled=True)  103 us
    unnamed x2, blocking collectives  95.1 us
    dot_general x8, matrix products, tile_scores(): jnp.einsum('ijk,kh->hij', kernels_low, kernel_heads, preferred_element_ty...  31.1 us
    psum x1, waiting for transfers between devices, body(): lax.psum(owned[3].astype(jnp.bfloat16), 'rep').astype(jnp.float32)  28.5 us
    dot_general x4, matrix products, one_tile(): jnp.einsum('ijk,hij->kh', kernels_low, grad_scores, preferred_element_typ...  24.7 us
    all_gather x1, blocking collectives, body(): lax.all_gather(bias_rows, 'fsdp', axis=1, tiled=True)  23.5 us
  transfers between devices with their start and end apart: 11, of which 5 were waited for; matrix products, arithmetic and copies ran while one was open for 32% of the time, Pallas kernels for 0%

commit v1 on v0

v1 whole, which is shorter than its diff:
```python
from functools import partial
import math

import jax
import jax.numpy as jnp
from jax import lax
from jax.sharding import Mesh, PartitionSpec as P
import numpy as np

ATOM_TYPES = 64


epsilon = 1e-05
masked_score = -1000000000.0
time_scale = 1000.0
root_two_pi = math.sqrt(2.0 * math.pi)
highest = lax.Precision.HIGHEST


def time_embedding(times, model_width):
    half_width = model_width // 2
    counter = jnp.arange(half_width, dtype=jnp.float32)
    frequency = jnp.exp(counter * (-math.log(10000.0) / half_width))
    angles = (time_scale * times)[:, None] * frequency[None, :]
    return jnp.concatenate([jnp.sin(angles), jnp.cos(angles)], axis=1)


def layer_norm(values, gain_row, shift_row):
    center = values - jnp.mean(values, axis=1, keepdims=True)
    inv_std = lax.rsqrt(jnp.mean(center * center, axis=1, keepdims=True) + epsilon)
    normed = center * inv_std
    return (normed * gain_row + shift_row, normed, inv_std)


def norm_backward(grad_out, normed, inv_std, gain_row):
    grad_normed = grad_out * gain_row
    first_mean = jnp.mean(grad_normed, axis=1, keepdims=True)
    second_mean = jnp.mean(grad_normed * normed, axis=1, keepdims=True)
    grad_input = inv_std * (grad_normed - first_mean - normed * second_mean)
    return (grad_input, jnp.sum(grad_out * normed, axis=0), jnp.sum(grad_out, axis=0))


def gelu_value(values):
    return values * (0.5 + 0.5 * lax.erf(values * math.sqrt(0.5)))


def gelu_slope(values):
    return (
        0.5
        + 0.5 * lax.erf(values * math.sqrt(0.5))
        + values * jnp.exp(-0.5 * values * values) / root_two_pi
    )


def pair_terms(pos_rows, pos_cols, type_rows, type_cols, tables):
    kernel_means, kernel_widths, scale_table, shift_table = tables
    offsets = pos_rows[:, :, None] - pos_cols[:, None, :]
    distance = jnp.sqrt(jnp.sum(offsets * offsets, axis=0))
    type_range = jnp.arange(ATOM_TYPES, dtype=jnp.int32)
    hot_rows = (type_rows[:, None] == type_range[None, :]).astype(jnp.float32)
    hot_cols = (type_cols[:, None] == type_range[None, :]).astype(jnp.float32)
    scale_pair = jnp.dot(
        jnp.dot(hot_rows, scale_table, precision=highest), hot_cols.T, precision=highest
    )
    shift_pair = jnp.dot(
        jnp.dot(hot_rows, shift_table, precision=highest), hot_cols.T, precision=highest
    )
    stretched = scale_pair * distance + shift_pair
    kernel_gap = (stretched[:, :, None] - kernel_means) / kernel_widths
    kernels = jnp.exp(-0.5 * kernel_gap * kernel_gap) / (root_two_pi * kernel_widths)
    return (distance, hot_rows, hot_cols, kernel_gap, kernels)


def allowed_pairs(row_ids, col_ids, mol_rows, mol_cols, pad_cols):
    same_mol = mol_rows[:, None] == mol_cols[None, :]
    key_live = (pad_cols[None, :] == 1) | (row_ids[:, None] == col_ids[None, :])
    return same_mol & key_live


def tile_scores(q_tile, key_block, kernels_low, kernel_heads, allowed, score_scale):
    pair_bias = jnp.einsum(
        "ijk,kh->hij", kernels_low, kernel_heads, preferred_element_type=jnp.float32
    )
    raw_scores = jnp.einsum("ihd,jhd->hij", q_tile, key_block, preferred_element_type=jnp.float32)
    return jnp.where(allowed[None], raw_scores * score_scale + pair_bias, masked_score)


def block_forward(pieces, tables, kernel_heads, tile_rows):
    queries, key_block, value_block, positions, types, mols, pads = pieces
    block_rows = queries.shape[0]
    score_scale = 1.0 / math.sqrt(queries.shape[2])
    col_ids = jnp.arange(block_rows, dtype=jnp.int32)

    def one_tile(running, tile_index):
        first_row = tile_index * tile_rows
        row_ids = first_row + jnp.arange(tile_rows, dtype=jnp.int32)
        terms = pair_terms(positions, positions, types, types, tables)
        kernels_low = terms[4].astype(jnp.bfloat16)
        allowed = allowed_pairs(row_ids, col_ids, mols, mols, pads)
        scores = tile_scores(queries, key_block, kernels_low, kernel_heads, allowed, score_scale)
        row_max = jnp.max(scores, axis=2, keepdims=True)
        exponent = jnp.exp(scores - row_max)
        row_sum = jnp.sum(exponent, axis=2, keepdims=True)
        probs_low = (exponent / row_sum).astype(jnp.bfloat16)
        attended = jnp.einsum(
            "hij,jhd->ihd", probs_low, value_block, preferred_element_type=jnp.float32
        )
        return (running, (attended, (row_max + jnp.log(row_sum))[:, :, 0]))

    count = block_rows // tile_rows
    if count == 1:
        _, (attended, log_sums) = one_tile(None, 0)
        return (attended.reshape(block_rows, -1), log_sums)
    _, (attended, log_sums) = lax.scan(one_tile, None, jnp.arange(count, dtype=jnp.int32))
    attended = attended.reshape(block_rows, -1)
    log_sums = jnp.transpose(log_sums, (1, 0, 2)).reshape(log_sums.shape[1], block_rows)
    return (attended, log_sums)


def block_backward(running, pieces, tables, kernel_heads, tile_rows):
    queries, key_block, value_block, grad_attended, log_sums, positions, types, mols, pads = pieces
    kernel_widths = tables[1]
    block_rows = queries.shape[0]
    score_scale = 1.0 / math.sqrt(queries.shape[2])
    col_ids = jnp.arange(block_rows, dtype=jnp.int32)

    def one_tile(partial_sums, tile_index):
        keys_grad, values_grad, heads_grad, means_grad, widths_grad, scale_grad, shift_grad = (
            partial_sums
        )
        first_row = tile_index * tile_rows
        row_ids = first_row + jnp.arange(tile_rows, dtype=jnp.int32)
        distance, hot_rows, hot_cols, kernel_gap, kernels = pair_terms(
            positions, positions, types, types, tables
        )
        kernels_low = kernels.astype(jnp.bfloat16)
        allowed = allowed_pairs(row_ids, col_ids, mols, mols, pads)
        scores = tile_scores(queries, key_block, kernels_low, kernel_heads, allowed, score_scale)
        attn_probs = jnp.exp(scores - log_sums[:, :, None])
        grad_probs = jnp.einsum(
            "ihd,jhd->hij", grad_attended, value_block, preferred_element_type=jnp.float32
        )
        values_grad = values_grad + jnp.einsum(
            "hij,ihd->jhd",
            attn_probs.astype(jnp.bfloat16),
            grad_attended,
            preferred_element_type=jnp.float32,
        )
        probs_dot = jnp.sum(attn_probs * grad_probs, axis=2, keepdims=True)
        grad_scores = (attn_probs * (grad_probs - probs_dot)).astype(jnp.bfloat16)
        query_grad = (
            jnp.einsum("hij,jhd->ihd", grad_scores, key_block, preferred_element_type=jnp.float32)
            * score_scale
        )
        keys_grad = (
            keys_grad
            + jnp.einsum("hij,ihd->jhd", grad_scores, queries, preferred_element_type=jnp.float32)
            * score_scale
        )
        heads_grad = heads_grad + jnp.einsum(
            "ijk,hij->kh", kernels_low, grad_scores, preferred_element_type=jnp.float32
        )
        grad_kernels = jnp.einsum(
            "hij,kh->ijk", grad_scores, kernel_heads, preferred_element_type=jnp.float32
        )
        spread = grad_kernels * kernels
        mean_part = spread * kernel_gap / kernel_widths
        means_grad = means_grad + jnp.sum(mean_part, axis=(0, 1))
        widths_grad = widths_grad + jnp.sum(
            spread * (kernel_gap * kernel_gap - 1.0) / kernel_widths, axis=(0, 1)
        )
        grad_stretched = -jnp.sum(mean_part, axis=2)
        scale_grad = scale_grad + jnp.dot(
            jnp.dot(hot_rows.T, grad_stretched * distance, precision=highest),
            hot_cols,
            precision=highest,
        )
        shift_grad = shift_grad + jnp.dot(
            jnp.dot(hot_rows.T, grad_stretched, precision=highest), hot_cols, precision=highest
        )
        return (
            (keys_grad, values_grad, heads_grad, means_grad, widths_grad, scale_grad, shift_grad),
            query_grad,
        )

    zero_block = jnp.zeros(key_block.shape, jnp.float32)
    count = block_rows // tile_rows
    if count == 1:
        sums_out, query_grads = one_tile((zero_block, zero_block) + tuple(running), 0)
        return (sums_out[2:], (query_grads.reshape(key_block.shape), sums_out[0], sums_out[1]))
    sums_out, query_grads = lax.scan(
        one_tile, (zero_block, zero_block) + tuple(running), jnp.arange(count, dtype=jnp.int32)
    )
    query_grads = query_grads.reshape(key_block.shape)
    return (sums_out[2:], (query_grads, sums_out[0], sums_out[1]))


def snake_ring(chips_x, chips_other):
    if chips_x == 2 and chips_other >= 2:
        return [2 * z for z in range(chips_other)] + [
            2 * z + 1 for z in reversed(range(chips_other))
        ]
    return list(range(chips_x * chips_other))


class Ring:
    def __init__(self, order):
        self.order = order
        self.n = len(order)
        pos = np.zeros(self.n, np.int32)
        for i, c in enumerate(order):
            pos[c] = i
        self.pos = pos
        self.cw = [(order[i], order[(i + 1) % self.n]) for i in range(self.n)]
        self.ccw = [(order[i], order[(i - 1) % self.n]) for i in range(self.n)]

    def here(self):
        chip = lax.axis_index("chip")
        core = lax.axis_index("core")
        return chip, core, jnp.asarray(self.pos)[chip]

    def chip_at(self, position):
        return jnp.asarray(np.array(self.order, np.int32))[position % self.n]


SWAP = [(0, 1), (1, 0)]


def _halves(x, axis):
    size = x.shape[axis] // 2
    return (
        lax.slice_in_dim(x, 0, size, axis=axis),
        lax.slice_in_dim(x, size, 2 * size, axis=axis),
    )


def ring_gather(ring, pieces, chips):
    if ring is None:
        return [
            lax.all_gather(x, ("chip", "core"), axis=0, tiled=False).reshape((chips, 2) + x.shape)
            for x, _ in pieces
        ]
    chip, core, p = ring.here()
    n = ring.n
    bufs, fronts = [], []
    for x, axis in pieces:
        buf = jnp.zeros((n, 2) + x.shape, x.dtype)
        buf = lax.dynamic_update_slice(buf, x[None, None], (chip, core) + (0,) * x.ndim)
        bufs.append(buf)
        if axis is None:
            fronts.append([x, None])
        else:
            fronts.append(list(_halves(x, axis)))
    partner = lax.ppermute([x for x, _ in pieces], "core", SWAP)
    for i, x in enumerate(partner):
        bufs[i] = lax.dynamic_update_slice(
            bufs[i], x[None, None], (chip, 1 - core) + (0,) * x.ndim
        )
    for step in range(1, n):
        going = [f[0] for f in fronts]
        coming = [f[1] for f in fronts if f[1] is not None]
        going = lax.ppermute(going, "chip", ring.cw)
        coming = lax.ppermute(coming, "chip", ring.ccw) if coming else []
        from_cw = ring.chip_at(p - step)
        from_ccw = ring.chip_at(p + step)
        both = lax.ppermute([going, coming], "core", SWAP)
        j = 0
        for i, (x, axis) in enumerate(pieces):
            fronts[i][0] = going[i]
            parts = [(going[i], both[0][i], from_cw, 0)]
            if axis is not None:
                fronts[i][1] = coming[j]
                parts.append((coming[j], both[1][j], from_ccw, x.shape[axis] // 2))
                j += 1
            for mine, theirs, source, offset in parts:
                start = [0] * x.ndim
                if axis is not None:
                    start[axis] = offset
                bufs[i] = lax.dynamic_update_slice(
                    bufs[i], mine[None, None], (source, core) + tuple(start)
                )
                bufs[i] = lax.dynamic_update_slice(
                    bufs[i], theirs[None, None], (source, 1 - core) + tuple(start)
                )
    return bufs


def ring_reduce(ring, pieces, send=jnp.bfloat16):
    if ring is None:
        owned = []
        for g, _ in pieces:
            flat = g.reshape((-1,) + g.shape[3:])
            part = lax.psum_scatter(flat, ("chip", "core"), scatter_dimension=0, tiled=True)
            owned.append(lax.psum(part.astype(send), "rep").astype(jnp.float32))
        return owned
    chip, core, p = ring.here()
    n = ring.n
    mine, theirs = [], []
    for g, _ in pieces:
        mine.append(lax.dynamic_index_in_dim(g, core, axis=1, keepdims=False))
        theirs.append(lax.dynamic_index_in_dim(g, 1 - core, axis=1, keepdims=False).astype(send))
    got = lax.ppermute(theirs, "core", SWAP)
    sums = [m + t.astype(jnp.float32) for m, t in zip(mine, got)]
    cw_parts, ccw_parts = [], []
    for (g, axis), total in zip(pieces, sums):
        if axis is None:
            cw_parts.append(total)
            ccw_parts.append(None)
        else:
            a, b = _halves(total, axis + 1)
            cw_parts.append(a)
            ccw_parts.append(b)

    def block(parts, position):
        return lax.dynamic_index_in_dim(parts, ring.chip_at(position), axis=0, keepdims=False)

    acc_cw = [block(t, p - 1) for t in cw_parts]
    acc_ccw = [block(t, p + 1) for t in ccw_parts if t is not None]
    for step in range(1, n):
        acc_cw = lax.ppermute([a.astype(send) for a in acc_cw], "chip", ring.cw)
        acc_cw = [a.astype(jnp.float32) + block(t, p - 1 - step) for a, t in zip(acc_cw, cw_parts)]
        if acc_ccw:
            acc_ccw = lax.ppermute([a.astype(send) for a in acc_ccw], "chip", ring.ccw)
            live = [t for t in ccw_parts if t is not None]
            acc_ccw = [a.astype(jnp.float32) + block(t, p + 1 + step) for a, t in zip(acc_ccw, live)]
    owned, j = [], 0
    for (g, axis), a in zip(pieces, acc_cw):
        if axis is None:
            owned.append(a)
        else:
            owned.append(jnp.concatenate([a, acc_ccw[j]], axis=axis))
            j += 1
    other = lax.ppermute([o.astype(send) for o in owned], "rep", SWAP)
    return [o + t.astype(jnp.float32) for o, t in zip(owned, other)]


SMALL_ROWS, SMALL_LANES = 16, 768


def small_layout(fsdp):
    d = 768 // fsdp
    sizes = [2 * d, 6 * d, 3072 // fsdp, 128 // fsdp, 128 // fsdp, 4096 // fsdp, 4096 // fsdp, (128 // fsdp) * 32]
    offsets, at = [], 0
    for size in sizes:
        offsets.append((at, size))
        at += size
    assert at <= SMALL_ROWS * SMALL_LANES
    return offsets


def pack_small(parts):
    flat = jnp.concatenate([part.reshape(-1) for part in parts])
    flat = jnp.pad(flat, (0, SMALL_ROWS * SMALL_LANES - flat.shape[0]))
    return flat.reshape(SMALL_ROWS, SMALL_LANES)


def unpack_small_full(gathered, offsets, fsdp):
    flat = gathered.reshape(fsdp, -1).astype(jnp.float32)
    take = [flat[:, at : at + size] for at, size in offsets]
    d = 768 // fsdp
    return [
        take[0].reshape(fsdp, 2, d).transpose(1, 0, 2).reshape(2, -1),
        take[1].reshape(fsdp, 6, d).transpose(1, 0, 2).reshape(6, -1),
        take[2].reshape(-1),
        take[3].reshape(-1),
        take[4].reshape(-1),
        take[5].reshape(ATOM_TYPES, ATOM_TYPES),
        take[6].reshape(ATOM_TYPES, ATOM_TYPES),
        take[7].reshape(-1, 32),
    ]


def pack_small_grads(grads, fsdp, chips):
    d = 768 // fsdp
    blocks = [
        grads[0].reshape(2, fsdp, d).transpose(1, 0, 2),
        grads[1].reshape(6, fsdp, d).transpose(1, 0, 2),
    ] + [g.reshape(-1) for g in grads[2:]]
    flat = jnp.concatenate([blk.reshape(fsdp, -1) for blk in blocks], axis=1)
    flat = jnp.pad(flat, ((0, 0), (0, SMALL_ROWS * SMALL_LANES - flat.shape[1])))
    return flat.reshape(chips, 2, SMALL_ROWS, SMALL_LANES)


def unpack_small_owned(block, offsets):
    flat = block.reshape(-1)
    take = [flat[at : at + size] for at, size in offsets]
    return [
        take[0].reshape(2, -1),
        take[1].reshape(6, -1),
        take[2],
        take[3],
        take[4],
        take[5],
        take[6],
        take[7].reshape(-1, 32),
    ]


def make_body(ring, chips):
    fsdp = 2 * chips

    def body(
        inputs,
        times,
        positions,
        atom_types,
        molecule_ids,
        pad_mask,
        cotangent,
        norm_gains,
        bias_rows,
        up_bias,
        input_weight,
        output_weight,
        up_weight,
        down_weight,
        kernel_means,
        kernel_widths,
        pair_scale,
        pair_shift,
        kernel_heads,
    ):
        offsets = small_layout(fsdp)
        small = pack_small(
            [norm_gains, bias_rows, up_bias, kernel_means, kernel_widths, pair_scale, pair_shift, kernel_heads]
        )
        width = input_weight.shape[0]
        first = jnp.concatenate([small.reshape(-1, width), input_weight.T], axis=0)
        second = jnp.concatenate(
            [output_weight.T, up_weight.T, down_weight.T.reshape(-1, width)], axis=0
        )
        first_all = lax.all_gather(first, ("chip", "core"), axis=0, tiled=False)
        second_all = lax.all_gather(second, ("chip", "core"), axis=0, tiled=False)
        small_rows = small.size // width
        params = unpack_small_full(first_all[:, :small_rows], offsets, fsdp)
        in_t = first_all[:, small_rows:].reshape(-1, width)
        out_rows = output_weight.shape[1]
        up_rows = up_weight.shape[1]
        out_t = second_all[:, :out_rows].reshape(-1, width)
        up_t = second_all[:, out_rows : out_rows + up_rows].reshape(-1, width)
        down_t = (
            second_all[:, out_rows + up_rows :]
            .reshape(fsdp, down_weight.shape[1], -1)
            .reshape(-1, down_weight.shape[0])
        )
        gains_now, biases_now, up_shift = params[0], params[1], params[2]
        tables = (params[3], params[4], params[5], params[6])
        heads_full = params[7].astype(jnp.bfloat16)

        row_count = inputs.shape[0]
        model_width = inputs.shape[1]
        head_count = heads_full.shape[1]
        head_size = model_width // head_count
        block_rows = min(128, row_count)
        blocks = row_count // block_rows
        tile_rows = min(128, block_rows)
        nt = (((1,), (1,)), ((), ()))
        tn = (((0,), (0,)), ((), ()))

        stream = inputs.astype(jnp.float32) + time_embedding(times, model_width)
        normed_out, normed_one, inv_one = layer_norm(stream, gains_now[0], biases_now[0])
        act_one = normed_out.astype(jnp.bfloat16)
        qkv_shift = jnp.concatenate([biases_now[2], jnp.zeros_like(biases_now[2]), biases_now[3]])
        projected = (
            lax.dot_general(act_one, in_t, nt, preferred_element_type=jnp.float32) + qkv_shift
        ).astype(jnp.bfloat16)
        split_shape = (blocks, block_rows, head_count, head_size)
        queries = projected[:, :model_width].reshape(split_shape)
        key_rows = projected[:, model_width : 2 * model_width].reshape(split_shape)
        value_rows = projected[:, 2 * model_width :].reshape(split_shape)
        pos_blocks = jnp.transpose(positions.reshape(3, blocks, block_rows), (1, 0, 2))
        type_blocks = atom_types.reshape(blocks, block_rows)
        mol_blocks = molecule_ids.reshape(blocks, block_rows)
        pad_blocks = pad_mask.reshape(blocks, block_rows)
        fwd = [
            block_forward(
                (queries[b], key_rows[b], value_rows[b], pos_blocks[b], type_blocks[b], mol_blocks[b], pad_blocks[b]),
                tables=tables,
                kernel_heads=heads_full,
                tile_rows=tile_rows,
            )
            for b in range(blocks)
        ]
        attended = jnp.stack([f[0] for f in fwd])
        log_sums = [f[1] for f in fwd]
        attended_low = attended.reshape(row_count, model_width).astype(jnp.bfloat16)
        mid = stream + (
            lax.dot_general(attended_low, out_t, nt, preferred_element_type=jnp.float32)
            + biases_now[4]
        )
        normed_out_two, normed_two, inv_two = layer_norm(mid, gains_now[1], biases_now[1])
        act_two = normed_out_two.astype(jnp.bfloat16)
        hidden_pre = (
            lax.dot_general(act_two, up_t, nt, preferred_element_type=jnp.float32) + up_shift
        )
        hidden_low = gelu_value(hidden_pre).astype(jnp.bfloat16)
        final = mid + (
            lax.dot_general(hidden_low, down_t, nt, preferred_element_type=jnp.float32)
            + biases_now[5]
        )
        rows_out = final.astype(jnp.bfloat16)

        grad_final = cotangent.astype(jnp.float32)
        down_grad_t = lax.dot_general(cotangent, hidden_low, tn, preferred_element_type=jnp.float32)
        grad_hidden = jnp.dot(cotangent, down_t, preferred_element_type=jnp.float32) * gelu_slope(
            hidden_pre
        )
        grad_hidden_low = grad_hidden.astype(jnp.bfloat16)
        up_grad_t = lax.dot_general(grad_hidden_low, act_two, tn, preferred_element_type=jnp.float32)
        up_bias_grad = jnp.sum(grad_hidden_low.astype(jnp.float32), axis=0)
        grad_act_two = jnp.dot(grad_hidden_low, up_t, preferred_element_type=jnp.float32)
        grad_norm_two, gain_two_grad, shift_two_grad = norm_backward(
            grad_act_two, normed_two, inv_two, gains_now[1]
        )
        grad_mid = grad_final + grad_norm_two
        grad_branch_low = grad_mid.astype(jnp.bfloat16)
        out_grad_t = lax.dot_general(
            grad_branch_low, attended_low, tn, preferred_element_type=jnp.float32
        )
        late_packed = jnp.concatenate(
            [
                out_grad_t.reshape(chips, 2, -1, model_width),
                up_grad_t.reshape(chips, 2, -1, model_width),
                down_grad_t.reshape(chips, 2, -1, model_width),
            ],
            axis=2,
        )
        (late_owned,) = ring_reduce(ring, [(late_packed, 1)])
        grad_attended = jnp.dot(grad_branch_low, out_t, preferred_element_type=jnp.float32).astype(
            jnp.bfloat16
        )
        kernel_count = tables[0].shape[0]
        start_sums = (
            jnp.zeros((kernel_count, head_count), jnp.float32),
            jnp.zeros((kernel_count,), jnp.float32),
            jnp.zeros((kernel_count,), jnp.float32),
            jnp.zeros((ATOM_TYPES, ATOM_TYPES), jnp.float32),
            jnp.zeros((ATOM_TYPES, ATOM_TYPES), jnp.float32),
        )
        kernel_sums = start_sums
        q_grads, k_grads, v_grads = [], [], []
        grad_attended_blocks = grad_attended.reshape(split_shape)
        for b in range(blocks):
            kernel_sums, (qg, kg, vg) = block_backward(
                kernel_sums,
                (
                    queries[b],
                    key_rows[b],
                    value_rows[b],
                    grad_attended_blocks[b],
                    log_sums[b],
                    pos_blocks[b],
                    type_blocks[b],
                    mol_blocks[b],
                    pad_blocks[b],
                ),
                tables=tables,
                kernel_heads=heads_full,
                tile_rows=tile_rows,
            )
            q_grads.append(qg)
            k_grads.append(kg)
            v_grads.append(vg)
        queries_grad = jnp.stack(q_grads)
        keys_grad = jnp.stack(k_grads)
        values_grad = jnp.stack(v_grads)
        grad_projected = jnp.concatenate(
            [
                queries_grad.reshape(row_count, model_width),
                keys_grad.reshape(row_count, model_width),
                values_grad.reshape(row_count, model_width),
            ],
            axis=1,
        ).astype(jnp.bfloat16)
        in_grad_t = lax.dot_general(grad_projected, act_one, tn, preferred_element_type=jnp.float32)
        grad_act_one = jnp.dot(grad_projected, in_t, preferred_element_type=jnp.float32)
        grad_norm_one, gain_one_grad, shift_one_grad = norm_backward(
            grad_act_one, normed_one, inv_one, gains_now[0]
        )
        inputs_grad = grad_mid + grad_norm_one
        projected_sums = jnp.sum(grad_projected.astype(jnp.float32), axis=0)
        heads_grad, means_grad, widths_grad, scale_grad, shift_grad = kernel_sums
        small_grads = [
            jnp.stack([gain_one_grad, gain_two_grad]),
            jnp.stack(
                [
                    shift_one_grad,
                    shift_two_grad,
                    projected_sums[:model_width],
                    projected_sums[2 * model_width :],
                    jnp.sum(grad_branch_low.astype(jnp.float32), axis=0),
                    jnp.sum(grad_final, axis=0),
                ]
            ),
            up_bias_grad,
            means_grad,
            widths_grad,
            scale_grad,
            shift_grad,
            heads_grad,
        ]
        in_owned, small_owned = ring_reduce(
            ring,
            [
                (in_grad_t.reshape((chips, 2, -1) + in_grad_t.shape[1:]), 1),
                (pack_small_grads(small_grads, fsdp, chips), None),
            ],
        )
        out_owned = late_owned[: out_rows]
        up_owned = late_owned[out_rows : out_rows + up_rows]
        down_owned = late_owned[out_rows + up_rows :].reshape(down_weight.shape[1], -1)
        sg = unpack_small_owned(small_owned, offsets)
        return (
            rows_out,
            inputs_grad,
            sg[0],
            sg[1],
            sg[2],
            in_owned.T,
            out_owned.T,
            up_owned.T,
            down_owned.T,
            sg[3],
            sg[4],
            sg[5],
            sg[6],
            sg[7],
        )

    return body


def solution(mesh):
    reps, fsdp = mesh.devices.shape
    chips = fsdp // 2
    grid = Mesh(mesh.devices.reshape(reps, chips, 2), ("rep", "chip", "core"))
    chips_x = 1
    try:
        coords = [tuple(d.coords) for d in mesh.devices[0, ::2]]
        xs = sorted({c[0] for c in coords})
        chips_x = len(xs)
        flat_ok = all(
            coords[i][0] == xs[i % chips_x] for i in range(chips)
        )
        if not flat_ok:
            chips_x = 1
    except Exception:
        chips_x = 1
    ring = None
    if chips <= 8:
        ring = Ring(snake_ring(chips_x, chips // chips_x))
    atoms = ("rep", "chip", "core")
    cols = ("chip", "core")
    placed = (
        P(atoms, None),
        P(atoms),
        P(None, atoms),
        P(atoms),
        P(atoms),
        P(atoms),
        P(atoms, None),
        P(None, cols),
        P(None, cols),
        P(cols),
        P(None, cols),
        P(None, cols),
        P(None, cols),
        P(None, cols),
        P(cols),
        P(cols),
        P(cols),
        P(cols),
        P(cols, None),
    )
    return jax.shard_map(
        make_body(ring, chips),
        mesh=grid,
        in_specs=placed,
        out_specs=(
            P(atoms, None),
            P(atoms, None),
            P(None, cols),
            P(None, cols),
            P(cols),
            P(None, cols),
            P(None, cols),
            P(None, cols),
            P(None, cols),
            P(cols),
            P(cols),
            P(cols),
            P(cols),
            P(cols, None),
        ),
        check_vma=False,
    )
```

time: 919 us -> 560 us (0.61)
  waiting for transfers between devices: 356 us -> 91.4 us
  blocking collectives: 196 us -> 0 us
  matrix products: 228 us -> 152 us
  local copies, waits for them, and re-layouts: 58.9 us -> 126 us
  starting transfers between devices: 0.61 us -> 41.6 us
  between operations: 18.3 us -> 57.6 us
  other arithmetic: 51.6 us -> 80 us
    reduce_scatter x4 -> x0, waiting for transfers between devices: 216 us -> none  [the longest x1 113 us: body(): lax.psum_scatter(down_grad, 'fsdp', scatter_dimension=1, tiled=True)]
    unnamed x13 -> x2, waiting for transfers between devices: 112 us -> 0.03 us
    all_gather x5 -> x0, blocking collectives: 96 us -> none  [the longest x1 23.5 us: body(): lax.all_gather(bias_rows, 'fsdp', axis=1, tiled=True)]
    unnamed x2 -> x0, blocking collectives: 95.1 us -> none
    ppermute x0 -> x41, waiting for transfers between devices: none -> 58.3 us  [the longest x21 38.5 us: ring_reduce(): acc_cw = lax.ppermute([a.astype(send) for a in acc_cw], 'chip', ring.cw)]
    ppermute x0 -> x41, starting transfers between devices: none -> 41.5 us  [the longest x21 21.5 us: ring_reduce(): acc_cw = lax.ppermute([a.astype(send) for a in acc_cw], 'chip', ring.cw)]
    slice x4 -> x39, local copies, waits for them, and re-layouts: 1.89 us -> 35.4 us  [the longest x1 8.28 us: body(): second_all[:, out_rows + up_rows:].reshape(fsdp, down_weight.shape[1], -1)]
    all_gather x4 -> x2, waiting for transfers between devices: 0.06 us -> 33.1 us  [the longest x1 21.8 us: body(): first_all = lax.all_gather(first, ('chip', 'core'), axis=0, tiled=False)]
  transfers between devices with their start and end apart: 11 -> 43, of which waited for: 5 -> 17; matrix products, arithmetic and copies ran while one was open for 32% -> 32% of each run, Pallas kernels for 0% -> 0%
where the time goes in v1:
time: 560 us; the launch traced here: 549 us
  matrix products  152 us (27%)
  local copies, waits for them, and re-layouts  126 us (22%)
  waiting for transfers between devices  91.4 us (16%)
  other arithmetic  80 us (14%)
  between operations  57.6 us (10%)
  starting transfers between devices  41.6 us (7%)
    ppermute x21, waiting for transfers between devices, ring_reduce(): acc_cw = lax.ppermute([a.astype(send) for a in acc_cw], 'chip', ring.cw)  38.5 us
    dot_general x4, matrix products, one_tile(): jnp.einsum('hij,kh->ijk', grad_scores, kernel_heads, preferred_element_ty...  26.2 us
    dot_general x4, matrix products, tile_scores(): jnp.einsum('ijk,kh->hij', kernels_low, kernel_heads, preferred_element_ty...  22.4 us
    all_gather x1, waiting for transfers between devices, body(): first_all = lax.all_gather(first, ('chip', 'core'), axis=0, tiled=False)  21.8 us
    ppermute x21, starting transfers between devices, ring_reduce(): acc_cw = lax.ppermute([a.astype(send) for a in acc_cw], 'chip', ring.cw)  21.5 us
    ppermute x14, starting transfers between devices, ring_reduce(): acc_ccw = lax.ppermute([a.astype(send) for a in acc_ccw], 'chip', ring.ccw)  16 us
    dot_general x4, matrix products, one_tile(): jnp.einsum('ijk,hij->kh', kernels_low, grad_scores, preferred_element_typ...  15.3 us
    concatenate x1, other arithmetic, body(): jnp.concatenate([out_grad_t.reshape(chips, 2, -1, model_width), up_grad_t...  15 us
  transfers between devices with their start and end apart: 43, of which 17 were waited for; matrix products, arithmetic and copies ran while one was open for 32% of the time, Pallas kernels for 0%

profile of v1, /device:TPU:0, one launch (start us, length us, event | category | flops | bytes accessed | tf_op | source)
XLA Modules:
  0.0 549.0 jit_solution(8853434957892432406)
XLA Ops:
  9.5 3.4 concatenate.34
  15.9 1.9 pad_maximum_fusion.6
  38.4 2.8 multiply_sine_fusion
  44.8 21.8 %all-gather.5.cloned.1.call-done = bf16[2560,768]{1,0:T(8,128)(2,1)} async-done(((bf16[160,768]{1,0:T(8,128)(2,1)}), bf16[2560,768]{1,0:T(8,128)(2,1)}) %all-gather.5.cloned.1.call-update) | async-done | bytes 3932176 | tf_op jit(solution)/shard_map/all_gather | solution.py:432
  67.6 4.0 slice.384
  77.3 5.6 %fusion.30 = f32[32,128,128]{2,0,1:T(8,128)} fusion(f32[128]{0:T(128)S(1)} %broadcast_multiply_fusion.7, f32[128]{0:T(128)S(1)} %div.76, f32[128]{0:T(128)S(1)} %sub.169, f32[128,128]{1,0:T(8,128)S(1)} %convolution_add_fusion.4, bf16[128,32]{1,0:T(8,128)(2,1)S(1)} %convert_element_type.407), kind=kOutput, calls=%fused_computation.55 | convolution fusion | flops 146800640 | bytes 2172416 | tf_op jit(solution)/shard_map/ijk,kh->hij/dot_general | solution.py:81
  83.0 3.0 copy.203
  87.0 5.6 %fusion.34 = f32[32,128,128]{2,0,1:T(8,128)} fusion(f32[128]{0:T(128)S(1)} %broadcast_multiply_fusion.7, f32[128]{0:T(128)S(1)} %div.76, f32[128]{0:T(128)S(1)} %sub.169, f32[128,128]{1,0:T(8,128)S(1)} %convolution_add_fusion.3, bf16[128,32]{1,0:T(8,128)(2,1)S(1)} %convert_element_type.407), kind=kOutput, calls=%fused_computation.57 | convolution fusion | flops 146800640 | bytes 2172416 | tf_op jit(solution)/shard_map/ijk,kh->hij/dot_general | solution.py:81
  92.6 3.0 copy.209
  96.6 5.6 %fusion.38 = f32[32,128,128]{2,0,1:T(8,128)} fusion(f32[128]{0:T(128)S(1)} %broadcast_multiply_fusion.7, f32[128]{0:T(128)S(1)} %div.76, f32[128]{0:T(128)S(1)} %sub.169, f32[128,128]{1,0:T(8,128)S(1)} %convolution_add_fusion.2, bf16[128,32]{1,0:T(8,128)(2,1)S(1)} %convert_element_type.407), kind=kOutput, calls=%fused_computation.59 | convolution fusion | flops 146800640 | bytes 2172416 | tf_op jit(solution)/shard_map/ijk,kh->hij/dot_general | solution.py:81
  102.2 3.0 copy.215
  107.0 5.6 %fusion.42 = f32[32,128,128]{2,0,1:T(8,128)} fusion(f32[128]{0:T(128)S(1)} %broadcast_multiply_fusion.7, f32[128]{0:T(128)S(1)} %div.76, f32[128]{0:T(128)S(1)} %sub.169, f32[128,128]{1,0:T(8,128)S(1)} %convolution_add_fusion.1, bf16[128,32]{1,0:T(8,128)(2,1)S(1)} %convert_element_type.407), kind=kOutput, calls=%fused_computation.61 | convolution fusion | flops 146800640 | bytes 2172416 | tf_op jit(solution)/shard_map/ijk,kh->hij/dot_general | solution.py:81
  112.6 3.2 copy.221
  115.9 4.2 fusion.19
  125.5 2.2 fusion.259
  130.5 2.0 copy-done.11
  133.5 1.9 copy-done.10
  145.2 11.3 %all-gather.7.cloned.1.call-done = bf16[6912,768]{1,0:T(8,128)(2,1)} async-done(((bf16[432,768]{1,0:T(8,128)(2,1)}), bf16[6912,768]{1,0:T(8,128)(2,1)}) %all-gather.7.cloned.1.call-update) | async-done | bytes 10616848 | tf_op jit(solution)/shard_map/all_gather | solution.py:433
  156.5 2.4 slice.408
  158.9 8.3 %fusion.245 = (bf16[16,192,768]{2,1,0:T(8,128)(2,1)}, bf16[16,192,768]{2,1,0:T(8,128)(2,1)}) fusion(bf16[16,432,768]{2,1,0:T(8,128)(2,1)} %bitcast.471), kind=kLoop, calls=%fused_computation.426 | loop fusion | bytes 18874368 | tf_op jit(solution)/shard_map/slice | solution.py:442
  167.2 8.5 %reshape_reshape.12 = bf16[768,3072]{1,0:T(8,128)(2,1)} reshape(bf16[16,192,768]{2,1,0:T(8,128)(2,1)} %get-tuple-element.48) | data formatting | bytes 9437184 | tf_op jit(solution)/shard_map/reshape;reshape | solution.py:444
  175.7 2.8 fusion.263
  179.0 4.9 multiply_convert_fusion
  183.9 5.4 convert_reduce_fusion
  189.3 3.5 multiply_reduce_fusion.4
  192.8 2.2 convert_bitcast_fusion
  196.8 3.1 fusion.62
  204.3 1.7 copy.245
  207.2 3.1 fusion.63
  214.3 1.9 copy.247
  217.4 2.1 fusion.64
  223.5 1.7 copy.249
  237.1 4.2 multiply_reduce_fusion.5
  242.7 5.8 %fusion.237 = f32[3072,768]{1,0:T(8,128)} fusion(bf16[512,3072]{1,0:T(8,128)(2,1)S(1)} %copy-done.146, f32[512,768]{1,0:T(8,128)S(1)} %copy-done.14, f32[768]{0:T(1024)S(1)} %copy-done.128, f32[768]{0:T(1024)S(1)} %copy-done.115, f32[512]{0:T(512)S(1)} %copy-done.123, f32[512]{0:T(512)S(1)} %copy-done.110), kind=kOutput, calls=%fused_computation.418 | convolution fusion | flops 2417885184 | bytes 14166016 | tf_op jit(solution)/shard_map/dot_general | solution.py:509
  248.6 3.0 fusion.73
  253.0 3.0 fusion.76
  257.3 3.0 fusion.79
  261.6 22.3 %fusion.9 = (f32[128]{0:T(128)}, f32[128]{0:T(128)}, f32[128]{0:T(128)}, f32[128]{0:T(128)}, f32[128,128,128]{2,1,0:T(8,128)}, /*index=5*/f32[128,128,128]{2,1,0...) fusion(f32[128,128]{1,0:T(8,128)S(1)} %copy-done.90, f32[128]{0:T(128)S(1)} %copy-done.141, ...), kind=kOutput, calls=%fused_computation.29 | convolution fusion | flops 243269120 | bytes 60042752 | tf_op jit(solution)/shard_map/hij,kh->ijk/dot_general | solution.py:163
  283.9 8.8 %fusion.241 = (f32[128,128]{1,0:T(8,128)S(1)}, f32[128]{0:T(128)}, f32[128]{0:T(128)}, f32[128,128]{1,0:T(8,128)S(1)}) fusion(f32[128,128,128]{2,1,0:T(8,128)} %get-tuple-element.53, f32[128,128,128]{2,1,0:T(8,128)} %get-tuple-element.50), kind=kLoop, calls=%fused_computation.422 | loop fusion | flops 8355584 | bytes 16909312 | tf_op jit(solution)/shard_map/reduce_sum | solution.py:172
  294.0 5.1 fusion.239
  300.8 6.3 %fusion.91 = f32[128,32]{0,1:T(8,128)S(1)} fusion(f32[128,32]{0,1:T(8,128)} %fusion.73, f32[128,32]{0,1:T(8,128)} %fusion.76, f32[128,32]{0,1:T(8,128)} %fusion.79, bf16[32,128,128]{2,0,1:T(8,128)(2,1)} %copy-done.19, f32[128]{0:T(128)} %copy-done.143, f32[128]{0:T(128)} %copy-done.140, f32[128]{0:T(128)} %copy-done.138, f32[128,128]{1,0:T(8,128)S(1)} %copy-done.88), kind=kOutput, calls=%fused_computation.177 | convolution fusion | flops 146812928 | bytes 1181184 | tf_op jit(solution)/shard_map/ijk,hij->kh/dot_general | solution.py:160
  308.9 3.1 convert_reduce_fusion.3
  317.0 8.3 %convolution_bitcast_fusion = f32[768,3072]{0,1:T(8,128)} fusion(bf16[512,3072]{1,0:T(8,128)(2,1)} %get-tuple-element.133, bf16[512,768]{1,0:T(8,128)(2,1)S(1)} %copy-done.51), kind=kOutput, calls=%fused_computation.41 | convolution fusion | flops 2415919104 | bytes 13369344 | tf_op jit(solution)/shard_map/dot_general | solution.py:504
  327.9 1.9 fusion.264
  329.8 9.8 %copy.258 = f32[768,3072]{1,0:T(8,128)} copy(f32[768,3072]{0,1:T(8,128)} %convolution_bitcast_fusion) | data formatting | bytes 18874368 | tf_op jit(solution)/shard_map/dot_general | solution.py:504
  339.6 11.5 %reshape.656 = f32[8,2,192,768]{3,2,1,0:T(8,128)} reshape(f32[768,3072]{1,0:T(8,128)} %copy.258) | data formatting | bytes 18874368 | tf_op jit(solution)/shard_map/reshape | solution.py:524
  353.2 15.0 %pad_maximum_fusion = f32[8,2,432,768]{3,2,1,0:T(8,128)} fusion(f32[8,2,192,768]{3,2,1,0:T(8,128)} %reshape.656, f32[8,2,192,768]{3,2,1,0:T(8,128)} %bitcast.472, f32[8,2,48,768]{3,2,1,0:T(8,128)S(1)} %fusion.264), kind=kLoop, calls=%fused_computation | loop fusion | flops 10616832 | bytes 42467328 | tf_op jit(solution)/shard_map/concatenate | solution.py:520
  368.9 6.8 %fusion.18 = bf16[8,432,768]{2,1,0:T(8,128)(2,1)} fusion(f32[8,2,432,768]{3,2,1,0:T(8,128)} %pad_maximum_fusion, s32[]{:T(128)S(6)} %select_n.349), kind=kLoop, calls=%fused_computation.42 | loop fusion | bytes 10616836 | tf_op jit(solution)/shard_map/convert_element_type | solution.py:301
  381.3 3.9 fusion.236
  410.9 6.8 %add_convert_fusion = bf16[512,768]{1,0:T(8,128)(2,1)} fusion(f32[512,768]{1,0:T(8,128)S(1)} %copy-done.15, bf16[512,3072]{1,0:T(8,128)(2,1)} %get-tuple-element.133, bf16[768,3072]{1,0:T(8,128)(2,1)} %reshape_reshape.12, f32[768]{0:T(1024)S(1)} %add.779), kind=kOutput, calls=%fused_computation.106 | convolution fusion | flops 2417098752 | bytes 10226688 | tf_op jit(solution)/shard_map/dot_general | solution.py:498
  421.7 2.9 bitcast_add_fusion.1
  427.0 2.8 collective-permute-done.17
  432.0 2.6 collective-permute-done.18
  436.8 2.6 collective-permute-done.19
  442.9 10.6 %bitcast_add_fusion = f32[8,432,768]{2,1,0:T(8,128)} fusion(bf16[8,432,768]{2,1,0:T(8,128)(2,1)} %collective-permute-done.25, f32[8,2,432,768]{3,2,1,0:T(8,128)} %pad_maximum_fusion, s32[]{:T(128)S(6)} %select_n.348), kind=kLoop, calls=%fused_computation.5 | loop fusion | flops 5308416 | bytes 26542084 | tf_op jit(solution)/shard_map/add | solution.py:303
  453.4 4.8 fusion.244
  462.8 4.9 collective-permute-done.26
  472.4 5.5 %collective-permute-done.27 = bf16[432,384]{1,0:T(8,128)(2,1)S(1)} collective-permute-done((bf16[432,384]{1,0:T(8,128)(2,1)S(1)}, bf16[432,384]{1,0:T(8,128)(2,1)S(1)}, u32[]{:S(2)}, u32[]{:S(2)}) %collective-permute-start.27) | collective-permute-done | bytes 331808 | tf_op jit(solution)/shard_map/ppermute | solution.py:320
  481.6 6.9 %collective-permute-done.28 = bf16[432,384]{1,0:T(8,128)(2,1)S(1)} collective-permute-done((bf16[432,384]{1,0:T(8,128)(2,1)S(1)}, bf16[432,384]{1,0:T(8,128)(2,1)S(1)}, u32[]{:S(2)}, u32[]{:S(2)}) %collective-permute-start.28) | collective-permute-done | bytes 331808 | tf_op jit(solution)/shard_map/ppermute | solution.py:320
  492.2 6.5 %collective-permute-done.29 = bf16[432,384]{1,0:T(8,128)(2,1)S(1)} collective-permute-done((bf16[432,384]{1,0:T(8,128)(2,1)S(1)}, bf16[432,384]{1,0:T(8,128)(2,1)S(1)}, u32[]{:S(2)}, u32[]{:S(2)}) %collective-permute-start.29) | collective-permute-done | bytes 331808 | tf_op jit(solution)/shard_map/ppermute | solution.py:320
  503.1 6.0 %collective-permute-done.30 = bf16[432,384]{1,0:T(8,128)(2,1)S(1)} collective-permute-done((bf16[432,384]{1,0:T(8,128)(2,1)S(1)}, bf16[432,384]{1,0:T(8,128)(2,1)S(1)}, u32[]{:S(2)}, u32[]{:S(2)}) %collective-permute-start.30) | collective-permute-done | bytes 331808 | tf_op jit(solution)/shard_map/ppermute | solution.py:320
  512.7 3.7 collective-permute-done.31
  518.8 4.9 collective-permute-done.32
  528.7 9.5 %collective-permute-done.24 = bf16[144,768]{1,0:T(8,128)(2,1)S(1)} collective-permute-done((bf16[144,768]{1,0:T(8,128)(2,1)S(1)}, bf16[144,768]{1,0:T(8,128)(2,1)S(1)}, u32[]{:S(2)}, u32[]{:S(2)}) %collective-permute-start.24) | collective-permute-done | bytes 221216 | tf_op jit(solution)/shard_map/ppermute | solution.py:333
  (623 shorter events, 147.0 us)
Async XLA Ops:
  7.2 27.9 %copy-start.134 = (f32[512]{0:T(512)S(1)}, f32[512]{0:T(512)}, u32[]{:S(2)}) copy-start(f32[512]{0:T(512)} %param.61) | copy-start | bytes 6148
  7.2 27.9 %copy-start.124 = (f32[3,512]{1,0:T(4,128)S(1)}, f32[3,512]{1,0:T(4,128)}, u32[]{:S(2)}) copy-start(f32[3,512]{1,0:T(4,128)} %param.62) | copy-start | bytes 18436
  7.2 59.3 %all-gather.5.cloned.1.call-start = ((), (), s32[]{:S(2)}) async-start(), calls=%async_computation | async-start | bytes 4177920 | tf_op jit(solution)/shard_map/all_gather | solution.py:432
  14.7 141.8 %all-gather.7.cloned.1.call-start = ((), (), s32[]{:S(2)}) async-start(), calls=%async_computation.1 | async-start | bytes 11280384 | tf_op jit(solution)/shard_map/all_gather | solution.py:433
  35.4 51.1 %copy-start.68 = (f32[128,128]{1,0:T(8,128)}, f32[128,128]{1,0:T(8,128)S(1)}, u32[]{:S(2)}) copy-start(f32[128,128]{1,0:T(8,128)S(1)} %multiply_reduce_fusion.14) | copy-start | bytes 196612
  35.5 60.5 %copy-start.64 = (f32[128,128]{1,0:T(8,128)}, f32[128,128]{1,0:T(8,128)S(1)}, u32[]{:S(2)}) copy-start(f32[128,128]{1,0:T(8,128)S(1)} %multiply_reduce_fusion.13) | copy-start | bytes 196612
  35.6 70.1 %copy-start.66 = (f32[128,128]{1,0:T(8,128)}, f32[128,128]{1,0:T(8,128)S(1)}, u32[]{:S(2)}) copy-start(f32[128,128]{1,0:T(8,128)S(1)} %multiply_reduce_fusion.12) | copy-start | bytes 196612
  35.8 41.0 %copy-start.70 = (f32[128,128]{1,0:T(8,128)}, f32[128,128]{1,0:T(8,128)S(1)}, u32[]{:S(2)}) copy-start(f32[128,128]{1,0:T(8,128)S(1)} %multiply_reduce_fusion.15) | copy-start | bytes 196612
  41.5 74.3 %copy-start.6 = (f32[512,768]{1,0:T(8,128)}, f32[512,768]{1,0:T(8,128)S(1)}, u32[]{:S(2)}) copy-start(f32[512,768]{1,0:T(8,128)S(1)} %get-tuple-element.45) | copy-start | bytes 4718596
  41.5 74.3 %copy-start.106 = (f32[512]{0:T(512)}, f32[512]{0:T(512)S(1)}, u32[]{:S(2)}) copy-start(f32[512]{0:T(512)S(1)} %broadcast_multiply_fusion.5) | copy-start | bytes 6148
  41.9 35.2 %copy-start.104 = (s32[128]{0:T(128)}, s32[128]{0:T(128)S(1)}, u32[]{:S(2)}) copy-start(s32[128]{0:T(128)S(1)} %get-tuple-element.103) | copy-start | bytes 1540
  41.9 44.8 %copy-start.102 = (s32[128]{0:T(128)}, s32[128]{0:T(128)S(1)}, u32[]{:S(2)}) copy-start(s32[128]{0:T(128)S(1)} %get-tuple-element.104) | copy-start | bytes 1540
  41.9 54.5 %copy-start.100 = (s32[128]{0:T(128)}, s32[128]{0:T(128)S(1)}, u32[]{:S(2)}) copy-start(s32[128]{0:T(128)S(1)} %get-tuple-element.106) | copy-start | bytes 1540
  41.9 64.2 %copy-start.98 = (s32[128]{0:T(128)}, s32[128]{0:T(128)S(1)}, u32[]{:S(2)}) copy-start(s32[128]{0:T(128)S(1)} %get-tuple-element.105) | copy-start | bytes 1540
  42.0 73.9 %copy-start.119 = (f32[512]{0:T(512)}, f32[512]{0:T(512)S(1)}, u32[]{:S(2)}) copy-start(f32[512]{0:T(512)S(1)} %add_rsqrt_fusion.1) | copy-start | bytes 6148
  72.7 43.2 %copy-start.111 = (f32[768]{0:T(1024)}, f32[768]{0:T(1024)S(1)}, u32[]{:S(2)}) copy-start(f32[768]{0:T(1024)S(1)} %mul.385) | copy-start | bytes 9220
  73.5 32.8 %copy-start.138 = (f32[128]{0:T(128)}, f32[128]{0:T(128)S(1)}, u32[]{:S(2)}) copy-start(f32[128]{0:T(128)S(1)} %sub.169) | copy-start | bytes 1540
  73.6 32.8 %copy-start.140 = (f32[128]{0:T(128)}, f32[128]{0:T(128)S(1)}, u32[]{:S(2)}) copy-start(f32[128]{0:T(128)S(1)} %div.76) | copy-start | bytes 1540
  74.0 32.4 %copy-start.72 = (bf16[128,32]{1,0:T(8,128)(2,1)}, bf16[128,32]{1,0:T(8,128)(2,1)S(1)}, u32[]{:S(2)}) copy-start(bf16[128,32]{1,0:T(8,128)(2,1)S(1)} %convert_element_type.407) | copy-start | bytes 24580
  75.5 40.4 %copy-start.125 = (f32[768]{0:T(1024)}, f32[768]{0:T(1024)S(1)}, u32[]{:S(2)}) copy-start(f32[768]{0:T(1024)S(1)} %add.754) | copy-start | bytes 9220
  76.3 30.1 %copy-start.143 = (f32[128]{0:T(128)}, f32[128]{0:T(128)S(1)}, u32[]{:S(2)}) copy-start(f32[128]{0:T(128)S(1)} %broadcast_multiply_fusion.7) | copy-start | bytes 1540
  144.5 55.4 %copy-start.78 = (f32[32,128]{1,0:T(8,128)}, f32[32,128]{1,0:T(8,128)S(1)}, u32[]{:S(2)}) copy-start(f32[32,128]{1,0:T(8,128)S(1)} %log_add_fusion.2) | copy-start | bytes 49156
  316.6 8.9 %collective-permute-start = (bf16[8,16,768]{2,1,0:T(8,128)(2,1)S(1)}, bf16[8,16,768]{2,1,0:T(8,128)(2,1)}, u32[]{:S(2)}, u32[]{:S(2)}) collective-permute-start(bf16[8,16,768]{2,1,0:T(8,128)(2,1)S(1)} %fusion.130), channel_id=1, source_target_pairs={{0,1},{1,0},{2,3},{3,2},{4,5},{5,4},{6,7},{7,6},{8,9},{9,8},{10,11... | collective-permute-start | bytes 589832 | tf_op jit(solution)/shard_map/ppermute | solution.py:302
  326.5 58.7 %copy-start.39 = (f32[8,16,768]{2,1,0:T(8,128)}, f32[8,16,768]{2,1,0:T(8,128)S(1)}, u32[]{:S(2)}) copy-start(f32[8,16,768]{2,1,0:T(8,128)S(1)} %bitcast_add_fusion.16) | copy-start | bytes 1179652
  327.2 23.9 %collective-permute-start.1 = (bf16[16,768]{1,0:T(8,128)(2,1)}, bf16[16,768]{1,0:T(8,128)(2,1)}, u32[]{:S(2)}, u32[]{:S(2)}) collective-permute-start(bf16[16,768]{1,0:T(8,128)(2,1)} %fusion.226), channel_id=1, source_target_pairs={{0,4},{4,8},{8,12},{12,14},{14,10},{10,6},{6,2},{2,0},{1,5},{5,9},... | collective-permute-start | bytes 73736 | tf_op jit(solution)/shard_map/ppermute | solution.py:320
  351.9 16.3 %collective-permute-start.2 = (bf16[16,768]{1,0:T(8,128)(2,1)S(1)}, bf16[16,768]{1,0:T(8,128)(2,1)S(1)}, u32[]{:S(2)}, u32[]{:S(2)}) collective-permute-start(bf16[16,768]{1,0:T(8,128)(2,1)S(1)} %fusion.180), channel_id=1, source_target_pairs={{0,4},{4,8},{8,12},{12,14},{14,10},{10,6},{6,2},{2,0},{1,5},{5,9},... | collective-permute-start | bytes 73736 | tf_op jit(solution)/shard_map/ppermute | solution.py:320
  368.2 7.6 %collective-permute-start.3 = (bf16[16,768]{1,0:T(8,128)(2,1)S(1)}, bf16[16,768]{1,0:T(8,128)(2,1)S(1)}, u32[]{:S(2)}, u32[]{:S(2)}) collective-permute-start(bf16[16,768]{1,0:T(8,128)(2,1)S(1)} %fusion.179), channel_id=1, source_target_pairs={{0,4},{4,8},{8,12},{12,14},{14,10},{10,6},{6,2},{2,0},{1,5},{5,9},... | collective-permute-start | bytes 73736 | tf_op jit(solution)/shard_map/ppermute | solution.py:320
  375.8 67.1 %collective-permute-start.25 = (bf16[8,432,768]{2,1,0:T(8,128)(2,1)}, bf16[8,432,768]{2,1,0:T(8,128)(2,1)}, u32[]{:S(2)}, u32[]{:S(2)}) collective-permute-start(bf16[8,432,768]{2,1,0:T(8,128)(2,1)} %fusion.18), channel_id=1, source_target_pairs={{0,1},{1,0},{2,3},{3,2},{4,5},{5,4},{6,7},{7,6},{8,9},{9,8},{10,11... | collective-permute-start | bytes 15925256 | tf_op jit(solution)/shard_map/ppermute | solution.py:302
  375.8 4.0 collective-permute-start.4
  379.8 5.5 collective-permute-start.5
  385.9 4.6 collective-permute-start.6
  388.3 33.4 %collective-permute-start.9 = (bf16[8,144,768]{2,1,0:T(8,128)(2,1)S(1)}, bf16[8,144,768]{2,1,0:T(8,128)(2,1)}, u32[]{:S(2)}, u32[]{:S(2)}) collective-permute-start(bf16[8,144,768]{2,1,0:T(8,128)(2,1)S(1)} %fusion.48), channel_id=1, source_target_pairs={{0,1},{1,0},{2,3},{3,2},{4,5},{5,4},{6,7},{7,6},{8,9},{9,8},{10,11... | collective-permute-start | bytes 5308424 | tf_op jit(solution)/shard_map/ppermute | solution.py:302
  391.2 17.4 %collective-permute-start.7 = (bf16[16,768]{1,0:T(8,128)(2,1)S(1)}, bf16[16,768]{1,0:T(8,128)(2,1)S(1)}, u32[]{:S(2)}, u32[]{:S(2)}) collective-permute-start(bf16[16,768]{1,0:T(8,128)(2,1)S(1)} %fusion.175), channel_id=1, source_target_pairs={{0,4},{4,8},{8,12},{12,14},{14,10},{10,6},{6,2},{2,0},{1,5},{5,9},... | collective-permute-start | bytes 73736 | tf_op jit(solution)/shard_map/ppermute | solution.py:320
  409.4 8.3 %collective-permute-start.8 = (bf16[16,768]{1,0:T(8,128)(2,1)S(1)}, bf16[16,768]{1,0:T(8,128)(2,1)S(1)}, u32[]{:S(2)}, u32[]{:S(2)}) collective-permute-start(bf16[16,768]{1,0:T(8,128)(2,1)S(1)} %fusion.225), channel_id=1, source_target_pairs={{0,16},{16,0},{1,17},{17,1},{2,18},{18,2},{3,19},{19,3},{4,20},{20... | collective-permute-start | bytes 73736 | tf_op jit(solution)/shard_map/ppermute | solution.py:333
  424.9 5.0 collective-permute-start.17
  426.3 5.0 collective-permute-start.10
  429.9 4.8 collective-permute-start.18
  431.3 4.8 collective-permute-start.11
  434.7 4.8 collective-permute-start.19
  436.1 5.4 collective-permute-start.12
  440.2 20.3 %collective-permute-start.20 = (bf16[144,384]{1,0:T(8,128)(2,1)}, bf16[144,384]{1,0:T(8,128)(2,1)}, u32[]{:S(2)}, u32[]{:S(2)}) collective-permute-start(bf16[144,384]{1,0:T(8,128)(2,1)} %fusion.121), channel_id=1, source_target_pairs={{0,2},{4,0},{8,4},{12,8},{14,12},{10,14},{6,10},{2,6},{1,3},{5,1},... | collective-permute-start | bytes 331784 | tf_op jit(solution)/shard_map/ppermute | solution.py:323
  442.2 28.0 %collective-permute-start.13 = (bf16[144,384]{1,0:T(8,128)(2,1)}, bf16[144,384]{1,0:T(8,128)(2,1)}, u32[]{:S(2)}, u32[]{:S(2)}) collective-permute-start(bf16[144,384]{1,0:T(8,128)(2,1)} %fusion.127), channel_id=1, source_target_pairs={{0,4},{4,8},{8,12},{12,14},{14,10},{10,6},{6,2},{2,0},{1,5},{5,9},... | collective-permute-start | bytes 331784 | tf_op jit(solution)/shard_map/ppermute | solution.py:320
  458.3 9.4 %collective-permute-start.26 = (bf16[432,384]{1,0:T(8,128)(2,1)S(1)}, bf16[432,384]{1,0:T(8,128)(2,1)S(1)}, u32[]{:S(2)}, u32[]{:S(2)}) collective-permute-start(bf16[432,384]{1,0:T(8,128)(2,1)S(1)} %fusion.116), channel_id=1, source_target_pairs={{0,4},{4,8},{8,12},{12,14},{14,10},{10,6},{6,2},{2,0},{1,5},{5,9},... | collective-permute-start | bytes 995336 | tf_op jit(solution)/shard_map/ppermute | solution.py:320
  459.6 9.5 %collective-permute-start.33 = (bf16[432,384]{1,0:T(8,128)(2,1)S(1)}, bf16[432,384]{1,0:T(8,128)(2,1)S(1)}, u32[]{:S(2)}, u32[]{:S(2)}) collective-permute-start(bf16[432,384]{1,0:T(8,128)(2,1)S(1)} %fusion.117), channel_id=1, source_target_pairs={{0,2},{4,0},{8,4},{12,8},{14,12},{10,14},{6,10},{2,6},{1,3},{5,1},... | collective-permute-start | bytes 995336 | tf_op jit(solution)/shard_map/ppermute | solution.py:323
  461.4 18.8 %collective-permute-start.21 = (bf16[144,384]{1,0:T(8,128)(2,1)S(1)}, bf16[144,384]{1,0:T(8,128)(2,1)S(1)}, u32[]{:S(2)}, u32[]{:S(2)}) collective-permute-start(bf16[144,384]{1,0:T(8,128)(2,1)S(1)} %fusion.120), channel_id=1, source_target_pairs={{0,2},{4,0},{8,4},{12,8},{14,12},{10,14},{6,10},{2,6},{1,3},{5,1},... | collective-permute-start | bytes 331784 | tf_op jit(solution)/shard_map/ppermute | solution.py:323
  467.7 10.2 %collective-permute-start.27 = (bf16[432,384]{1,0:T(8,128)(2,1)S(1)}, bf16[432,384]{1,0:T(8,128)(2,1)S(1)}, u32[]{:S(2)}, u32[]{:S(2)}) collective-permute-start(bf16[432,384]{1,0:T(8,128)(2,1)S(1)} %fusion.114), channel_id=1, source_target_pairs={{0,4},{4,8},{8,12},{12,14},{14,10},{10,6},{6,2},{2,0},{1,5},{5,9},... | collective-permute-start | bytes 995336 | tf_op jit(solution)/shard_map/ppermute | solution.py:320
  469.1 10.2 %collective-permute-start.34 = (bf16[432,384]{1,0:T(8,128)(2,1)S(1)}, bf16[432,384]{1,0:T(8,128)(2,1)S(1)}, u32[]{:S(2)}, u32[]{:S(2)}) collective-permute-start(bf16[432,384]{1,0:T(8,128)(2,1)S(1)} %fusion.108), channel_id=1, source_target_pairs={{0,2},{4,0},{8,4},{12,8},{14,12},{10,14},{6,10},{2,6},{1,3},{5,1},... | collective-permute-start | bytes 995336 | tf_op jit(solution)/shard_map/ppermute | solution.py:323
  471.1 19.9 %collective-permute-start.14 = (bf16[144,384]{1,0:T(8,128)(2,1)S(1)}, bf16[144,384]{1,0:T(8,128)(2,1)S(1)}, u32[]{:S(2)}, u32[]{:S(2)}) collective-permute-start(bf16[144,384]{1,0:T(8,128)(2,1)S(1)} %fusion.126), channel_id=1, source_target_pairs={{0,4},{4,8},{8,12},{12,14},{14,10},{10,6},{6,2},{2,0},{1,5},{5,9},... | collective-permute-start | bytes 331784 | tf_op jit(solution)/shard_map/ppermute | solution.py:320
  478.0 10.5 %collective-permute-start.28 = (bf16[432,384]{1,0:T(8,128)(2,1)S(1)}, bf16[432,384]{1,0:T(8,128)(2,1)S(1)}, u32[]{:S(2)}, u32[]{:S(2)}) collective-permute-start(bf16[432,384]{1,0:T(8,128)(2,1)S(1)} %fusion.113), channel_id=1, source_target_pairs={{0,4},{4,8},{8,12},{12,14},{14,10},{10,6},{6,2},{2,0},{1,5},{5,9},... | collective-permute-start | bytes 995336 | tf_op jit(solution)/shard_map/ppermute | solution.py:320
  479.3 10.6 %collective-permute-start.35 = (bf16[432,384]{1,0:T(8,128)(2,1)S(1)}, bf16[432,384]{1,0:T(8,128)(2,1)S(1)}, u32[]{:S(2)}, u32[]{:S(2)}) collective-permute-start(bf16[432,384]{1,0:T(8,128)(2,1)S(1)} %fusion.107), channel_id=1, source_target_pairs={{0,2},{4,0},{8,4},{12,8},{14,12},{10,14},{6,10},{2,6},{1,3},{5,1},... | collective-permute-start | bytes 995336 | tf_op jit(solution)/shard_map/ppermute | solution.py:323
  480.3 21.5 %collective-permute-start.22 = (bf16[144,384]{1,0:T(8,128)(2,1)S(1)}, bf16[144,384]{1,0:T(8,128)(2,1)S(1)}, u32[]{:S(2)}, u32[]{:S(2)}) collective-permute-start(bf16[144,384]{1,0:T(8,128)(2,1)S(1)} %fusion.119), channel_id=1, source_target_pairs={{0,2},{4,0},{8,4},{12,8},{14,12},{10,14},{6,10},{2,6},{1,3},{5,1},... | collective-permute-start | bytes 331784 | tf_op jit(solution)/shard_map/ppermute | solution.py:323
  488.6 10.1 %collective-permute-start.29 = (bf16[432,384]{1,0:T(8,128)(2,1)S(1)}, bf16[432,384]{1,0:T(8,128)(2,1)S(1)}, u32[]{:S(2)}, u32[]{:S(2)}) collective-permute-start(bf16[432,384]{1,0:T(8,128)(2,1)S(1)} %fusion.112), channel_id=1, source_target_pairs={{0,4},{4,8},{8,12},{12,14},{14,10},{10,6},{6,2},{2,0},{1,5},{5,9},... | collective-permute-start | bytes 995336 | tf_op jit(solution)/shard_map/ppermute | solution.py:320
  490.0 10.7 %collective-permute-start.36 = (bf16[432,384]{1,0:T(8,128)(2,1)S(1)}, bf16[432,384]{1,0:T(8,128)(2,1)S(1)}, u32[]{:S(2)}, u32[]{:S(2)}) collective-permute-start(bf16[432,384]{1,0:T(8,128)(2,1)S(1)} %fusion.106), channel_id=1, source_target_pairs={{0,2},{4,0},{8,4},{12,8},{14,12},{10,14},{6,10},{2,6},{1,3},{5,1},... | collective-permute-start | bytes 995336 | tf_op jit(solution)/shard_map/ppermute | solution.py:323
  491.0 20.5 %collective-permute-start.15 = (bf16[144,384]{1,0:T(8,128)(2,1)S(1)}, bf16[144,384]{1,0:T(8,128)(2,1)S(1)}, u32[]{:S(2)}, u32[]{:S(2)}) collective-permute-start(bf16[144,384]{1,0:T(8,128)(2,1)S(1)} %fusion.125), channel_id=1, source_target_pairs={{0,4},{4,8},{8,12},{12,14},{14,10},{10,6},{6,2},{2,0},{1,5},{5,9},... | collective-permute-start | bytes 331784 | tf_op jit(solution)/shard_map/ppermute | solution.py:320
  498.8 10.4 %collective-permute-start.30 = (bf16[432,384]{1,0:T(8,128)(2,1)S(1)}, bf16[432,384]{1,0:T(8,128)(2,1)S(1)}, u32[]{:S(2)}, u32[]{:S(2)}) collective-permute-start(bf16[432,384]{1,0:T(8,128)(2,1)S(1)} %fusion.111), channel_id=1, source_target_pairs={{0,4},{4,8},{8,12},{12,14},{14,10},{10,6},{6,2},{2,0},{1,5},{5,9},... | collective-permute-start | bytes 995336 | tf_op jit(solution)/shard_map/ppermute | solution.py:320
  500.8 9.6 %collective-permute-start.37 = (bf16[432,384]{1,0:T(8,128)(2,1)S(1)}, bf16[432,384]{1,0:T(8,128)(2,1)S(1)}, u32[]{:S(2)}, u32[]{:S(2)}) collective-permute-start(bf16[432,384]{1,0:T(8,128)(2,1)S(1)} %fusion.105), channel_id=1, source_target_pairs={{0,2},{4,0},{8,4},{12,8},{14,12},{10,14},{6,10},{2,6},{1,3},{5,1},... | collective-permute-start | bytes 995336 | tf_op jit(solution)/shard_map/ppermute | solution.py:323
  501.8 17.0 %collective-permute-start.23 = (bf16[144,384]{1,0:T(8,128)(2,1)S(1)}, bf16[144,384]{1,0:T(8,128)(2,1)S(1)}, u32[]{:S(2)}, u32[]{:S(2)}) collective-permute-start(bf16[144,384]{1,0:T(8,128)(2,1)S(1)} %fusion.118), channel_id=1, source_target_pairs={{0,2},{4,0},{8,4},{12,8},{14,12},{10,14},{6,10},{2,6},{1,3},{5,1},... | collective-permute-start | bytes 331784 | tf_op jit(solution)/shard_map/ppermute | solution.py:323
  509.2 7.2 %collective-permute-start.31 = (bf16[432,384]{1,0:T(8,128)(2,1)S(1)}, bf16[432,384]{1,0:T(8,128)(2,1)S(1)}, u32[]{:S(2)}, u32[]{:S(2)}) collective-permute-start(bf16[432,384]{1,0:T(8,128)(2,1)S(1)} %fusion.110), channel_id=1, source_target_pairs={{0,4},{4,8},{8,12},{12,14},{14,10},{10,6},{6,2},{2,0},{1,5},{5,9},... | collective-permute-start | bytes 995336 | tf_op jit(solution)/shard_map/ppermute | solution.py:320
  510.6 7.2 %collective-permute-start.38 = (bf16[432,384]{1,0:T(8,128)(2,1)S(1)}, bf16[432,384]{1,0:T(8,128)(2,1)S(1)}, u32[]{:S(2)}, u32[]{:S(2)}) collective-permute-start(bf16[432,384]{1,0:T(8,128)(2,1)S(1)} %fusion.104), channel_id=1, source_target_pairs={{0,2},{4,0},{8,4},{12,8},{14,12},{10,14},{6,10},{2,6},{1,3},{5,1},... | collective-permute-start | bytes 995336 | tf_op jit(solution)/shard_map/ppermute | solution.py:323
  511.5 14.6 %collective-permute-start.16 = (bf16[144,384]{1,0:T(8,128)(2,1)S(1)}, bf16[144,384]{1,0:T(8,128)(2,1)S(1)}, u32[]{:S(2)}, u32[]{:S(2)}) collective-permute-start(bf16[144,384]{1,0:T(8,128)(2,1)S(1)} %fusion.124), channel_id=1, source_target_pairs={{0,4},{4,8},{8,12},{12,14},{14,10},{10,6},{6,2},{2,0},{1,5},{5,9},... | collective-permute-start | bytes 331784 | tf_op jit(solution)/shard_map/ppermute | solution.py:320
  516.5 7.2 %collective-permute-start.32 = (bf16[432,384]{1,0:T(8,128)(2,1)S(1)}, bf16[432,384]{1,0:T(8,128)(2,1)S(1)}, u32[]{:S(2)}, u32[]{:S(2)}) collective-permute-start(bf16[432,384]{1,0:T(8,128)(2,1)S(1)} %fusion.109), channel_id=1, source_target_pairs={{0,4},{4,8},{8,12},{12,14},{14,10},{10,6},{6,2},{2,0},{1,5},{5,9},... | collective-permute-start | bytes 995336 | tf_op jit(solution)/shard_map/ppermute | solution.py:320
  517.8 7.2 %collective-permute-start.39 = (bf16[432,384]{1,0:T(8,128)(2,1)S(1)}, bf16[432,384]{1,0:T(8,128)(2,1)S(1)}, u32[]{:S(2)}, u32[]{:S(2)}) collective-permute-start(bf16[432,384]{1,0:T(8,128)(2,1)S(1)} %fusion.103), channel_id=1, source_target_pairs={{0,2},{4,0},{8,4},{12,8},{14,12},{10,14},{6,10},{2,6},{1,3},{5,1},... | collective-permute-start | bytes 995336 | tf_op jit(solution)/shard_map/ppermute | solution.py:323
  525.1 13.9 %collective-permute-start.40 = (bf16[432,768]{1,0:T(8,128)(2,1)S(1)}, bf16[432,768]{1,0:T(8,128)(2,1)S(1)}, u32[]{:S(2)}, u32[]{:S(2)}) collective-permute-start(bf16[432,768]{1,0:T(8,128)(2,1)S(1)} %fusion.94), channel_id=1, source_target_pairs={{0,16},{16,0},{1,17},{17,1},{2,18},{18,2},{3,19},{19,3},{4,20},{20... | collective-permute-start | bytes 1990664 | tf_op jit(solution)/shard_map/ppermute | solution.py:333
  526.1 12.1 %collective-permute-start.24 = (bf16[144,768]{1,0:T(8,128)(2,1)S(1)}, bf16[144,768]{1,0:T(8,128)(2,1)S(1)}, u32[]{:S(2)}, u32[]{:S(2)}) collective-permute-start(bf16[144,768]{1,0:T(8,128)(2,1)S(1)} %fusion.115), channel_id=1, source_target_pairs={{0,16},{16,0},{1,17},{17,1},{2,18},{18,2},{3,19},{19,3},{4,20},{20... | collective-permute-start | bytes 663560 | tf_op jit(solution)/shard_map/ppermute | solution.py:333
  (128 other events, 653.4 us)
Sparse Core Ops, SparseCore 0:
  14.8 51.7 all-gather.4
  69.4 87.0 all-gather.6
